TPU v7x, 512 devices: a whole 4x8x8 slice. The times are simulated.
512 devices in a mesh: grp: 16 (over y, core), dom: 32 (over x, z).
Axes of the slice: x: 4, y: 8, z: 8, core: 2. Of those that a mesh axis runs over, the one named last changes fastest.
Arguments:
- owned_blips: bfloat16 [2048, 32768], P(('grp', 'dom')), may hold values from -6 to 6
- potential: float32 [32, 512, 1024], P('dom', 'grp'), may hold values from -5 to 5
- slot_owner: int32 [12288, 1], P(('grp', 'dom')), may hold values from 0 to 31; in each aligned block of 24 rows (0 to 23, 24 to 47, ...) at most 2 rows name the same one
- slot_row: int32 [12288], P(('grp', 'dom')), may hold values from 0 to 3
- slot_offset: int32 [12288], P(('grp', 'dom')), may hold values from 0 to 31
Outputs:
- blip_gradient: float32 [2048, 32768], P(('grp', 'dom'))
- hamiltonian: float32 [2048, 128], P(('grp', 'dom'))
Inputs may be any that keep to these rules, and one draw needn't show every extreme that they name: `slot_owner`: among the 24 pieces of one device at most 2 name the same owner.
All inputs are finite; a program needn't handle non-finite values.
Results may differ from a plain program's by a relative error of at most 0.012.
The roundings to bfloat16 on the way count: a program that leaves them out, or rounds other values in their place, can miss the bound.
Values may be sent and summed in bfloat16 or wider, within the bound.
No kernel may reach another device: no remote copies, remote signals or barrier semaphores. Data moves between devices by JAX's collectives and lax.ppermute only.
A program may use at most 128 MiB of HBM per device.

v0:
```python
import jax
import jax.numpy as jnp
from jax import lax
from jax.sharding import PartitionSpec as P

NB = 32


def passed_along(block, axis, distance):
    devices = range(lax.axis_size(axis))
    route = [((i - distance) % len(devices), i) for i in devices]
    return lax.ppermute(block, axis, route)


def spline_tables():
    cells_line = jnp.arange(NB, dtype=jnp.int32)
    offset = cells_line[:, None] - cells_line[None, :]
    spline = jnp.where(
        offset == 0, 2.0 / 3.0, jnp.where(jnp.abs(offset) == 1, 1.0 / 6.0, 0.0)
    ).astype(jnp.float32)
    second = jnp.where(offset == 0, -2.0, jnp.where(jnp.abs(offset) == 1, 1.0, 0.0)).astype(
        jnp.float32
    )
    plane_value = jnp.einsum("ac,bd->abcd", spline, spline).reshape(NB * NB, NB * NB)
    plane_curve = (
        jnp.einsum("ac,bd->abcd", second, spline) + jnp.einsum("ac,bd->abcd", spline, second)
    ).reshape(NB * NB, NB * NB)
    return (
        spline.astype(jnp.bfloat16),
        second.astype(jnp.bfloat16),
        plane_value.astype(jnp.bfloat16),
        plane_curve.astype(jnp.bfloat16),
    )


def on_device(owned_blips, potential, slot_owner, slot_row, slot_offset):
    spline, second, plane_value, plane_curve = spline_tables()
    domain_count = lax.axis_size("dom")
    slot_count = slot_row.shape[0]
    owned_count = owned_blips.shape[0]
    cell_count = owned_blips.shape[1]
    plane_cells = NB * NB
    capacity = max(2, -(-slot_count // domain_count))
    group_size = domain_count * owned_count
    owner_of = slot_owner[:, 0]
    target = owner_of * owned_count + slot_row
    owner_hot = (owner_of[:, None] == jnp.arange(domain_count, dtype=jnp.int32)[None, :]).astype(
        jnp.int32
    )
    position = jnp.sum(jnp.cumsum(owner_hot, axis=0) * owner_hot, axis=1) - 1
    place_slot = owner_of * capacity + position
    place_hot = place_slot[None, :] == jnp.arange(domain_count * capacity, dtype=jnp.int32)[:, None]
    asked_rows = jnp.sum(jnp.where(place_hot, slot_row[None, :], 0), axis=1) + owned_count * (
        1 - jnp.sum(place_hot.astype(jnp.int32), axis=1)
    )
    place_low = place_hot.astype(jnp.bfloat16)
    gathered_rows = lax.all_gather(owned_blips, "dom", axis=0, tiled=True)
    chosen = (
        target[:, None] == jnp.arange(gathered_rows.shape[0], dtype=jnp.int32)[None, :]
    ).astype(jnp.bfloat16)
    slot_blips = jnp.dot(chosen, gathered_rows, preferred_element_type=jnp.float32).astype(
        jnp.bfloat16
    )
    upper_cells = passed_along(potential, "grp", -1)
    extended = jnp.concatenate([potential[0], upper_cells[0]], axis=0)

    def cut_window(first_row):
        return lax.dynamic_slice_in_dim(extended, first_row, NB, 0)

    window = jax.vmap(cut_window)(slot_offset)
    layered = slot_blips.reshape(slot_count, NB, plane_cells)
    y_value = jnp.einsum("ya,sab->syb", spline, layered, preferred_element_type=jnp.float32).astype(
        jnp.bfloat16
    )
    y_curve = jnp.einsum("ya,sab->syb", second, layered, preferred_element_type=jnp.float32).astype(
        jnp.bfloat16
    )
    flat_value = y_value.reshape(-1, plane_cells)
    values_grid = jnp.dot(flat_value, plane_value, preferred_element_type=jnp.float32)
    laplace = jnp.dot(
        y_curve.reshape(-1, plane_cells), plane_value, preferred_element_type=jnp.float32
    ) + jnp.dot(flat_value, plane_curve, preferred_element_type=jnp.float32)
    applied = (-0.5 * laplace + window.reshape(-1, plane_cells) * values_grid).astype(jnp.bfloat16)
    values_low = values_grid.astype(jnp.bfloat16)
    back_plane = jnp.dot(applied, plane_value, preferred_element_type=jnp.float32).astype(
        jnp.bfloat16
    )
    gradient_piece = jnp.einsum(
        "ay,sab->syb",
        spline,
        back_plane.reshape(slot_count, NB, plane_cells),
        preferred_element_type=jnp.float32,
    ).astype(jnp.bfloat16)
    intersection = lax.dot_general(
        values_low.reshape(slot_count, cell_count),
        applied.reshape(slot_count, cell_count),
        (((1,), (1,)), ((), ())),
        preferred_element_type=jnp.float32,
    ) / float(cell_count)
    select_full = (target[:, None] == jnp.arange(group_size, dtype=jnp.int32)[None, :]).astype(
        jnp.float32
    )
    weighted = jnp.dot(intersection, select_full, precision=lax.Precision.HIGHEST)
    part_hot = (
        target[:, None] == jnp.arange(owned_count * lax.axis_size("dom"), dtype=jnp.int32)[None, :]
    ).astype(jnp.float32)
    hamilton = lax.psum_scatter(
        jnp.dot(part_hot.T, weighted, precision=lax.Precision.HIGHEST),
        "dom",
        scatter_dimension=0,
        tiled=True,
    )
    send_grad = jnp.dot(
        place_low,
        gradient_piece.reshape(slot_count, cell_count),
        preferred_element_type=jnp.bfloat16,
    ).reshape(domain_count, capacity, cell_count)
    got_grad, got_rows = (
        lax.all_to_all(send_grad, "dom", split_axis=0, concat_axis=0, tiled=True),
        lax.all_to_all(
            asked_rows.reshape(domain_count, capacity),
            "dom",
            split_axis=0,
            concat_axis=0,
            tiled=True,
        ),
    )
    owner_pick = (
        got_rows.reshape(-1)[None, :] == jnp.arange(owned_count, dtype=jnp.int32)[:, None]
    ).astype(jnp.bfloat16)
    gradient = jnp.dot(
        owner_pick, got_grad.reshape(-1, cell_count), preferred_element_type=jnp.float32
    )
    return (gradient, hamilton)


def solution(mesh):
    placed = (
        P(("grp", "dom"), None),
        P("dom", "grp", None),
        P(("grp", "dom"), None),
        P(("grp", "dom")),
        P(("grp", "dom")),
    )
    return jax.shard_map(
        on_device,
        mesh=mesh,
        in_specs=placed,
        out_specs=(P(("grp", "dom"), None), P(("grp", "dom"), None)),
        check_vma=False,
    )
```

profile of v0, /device:TPU:10, one launch (start us, length us, event | category | flops | bytes accessed | tf_op | source)
XLA Modules:
  0.0 352.6 jit_solution(15724551003374242884)
XLA Ops:
  11.7 13.5 %all-to-all-start = ((s32[32,1,2]{2,1,0:T(1,128)}), s32[32,1,2]{2,1,0:T(1,128)S(1)}, u32[]{:S(2)}, u32[]{:S(2)}) async-start(s32[32,1,2]{2,1,0:T(1,128)} %bitcast.1), calls=%async_computation | async-start | bytes 32768 | tf_op jit(solution)/shard_map/all_to_all | solution.py:120
  25.3 7.5 %fusion.1 = (bf16[32,32,32,32]{3,2,1,0:T(8,128)(2,1)}, bf16[32,32,32,32]{3,2,1,0:T(8,128)(2,1)}) fusion(f32[32,32]{1,0:T(8,128)S(1)} %copy.33, f32[32,32]{1,0:T(8,128)S(1)} %copy.30), kind=kLoop, calls=%fused_computation.6 | loop fusion | flops 6291456 | bytes 4202496 | tf_op jit(solution)/shard_map/convert_element_type | solution.py:32
  32.9 12.4 %convert_element_type.78 = bf16[1024,1024]{1,0:T(8,128)(2,1)} reshape(bf16[32,32,32,32]{3,2,1,0:T(8,128)(2,1)} %get-tuple-element.21) | data formatting | bytes 4194304 | tf_op jit(solution)/shard_map/convert_element_type | solution.py:31
  45.3 11.4 %convert_element_type.84 = bf16[1024,1024]{1,0:T(8,128)(2,1)S(1)} reshape(bf16[32,32,32,32]{3,2,1,0:T(8,128)(2,1)} %get-tuple-element.20) | data formatting | bytes 4194304 | tf_op jit(solution)/shard_map/convert_element_type | solution.py:32
  56.8 48.0 %while.1 = (s32[]{:T(128)}, f32[64,1024]{1,0:T(8,128)S(1)}, s32[24,2]{0,1:T(2,128)S(1)}, f32[24,32,1024]{2,1,0:T(8,128)}, s32[]{:T(128)}) while((s32[]{:T(128)}, f32[64,1024]{1,0:T(8,128)S(1)}, s32[24,2]{0,1:T(2,128)S(1)}, f32[24,32,1024]{2,1,0:T(8,128)}, s32[]{:T(128)}) %tuple.24), condition=%wide.while_cond, body=%wide.while_body.sunk | while | flops 2 | bytes 263257 | solution.py:68
  57.4 1.3 bitcast_dynamic-update-slice_fusion.2
  59.4 1.3 bitcast_dynamic-update-slice_fusion.2
  61.4 1.3 bitcast_dynamic-update-slice_fusion.2
  63.4 1.4 bitcast_dynamic-update-slice_fusion.2
  65.5 1.3 bitcast_dynamic-update-slice_fusion.2
  67.4 1.3 bitcast_dynamic-update-slice_fusion.2
  69.5 1.3 bitcast_dynamic-update-slice_fusion.2
  71.4 1.3 bitcast_dynamic-update-slice_fusion.2
  73.4 1.3 bitcast_dynamic-update-slice_fusion.2
  75.4 1.3 bitcast_dynamic-update-slice_fusion.2
  77.4 1.3 bitcast_dynamic-update-slice_fusion.2
  79.4 1.4 bitcast_dynamic-update-slice_fusion.2
  81.4 1.3 bitcast_dynamic-update-slice_fusion.2
  83.4 1.3 bitcast_dynamic-update-slice_fusion.2
  85.4 1.3 bitcast_dynamic-update-slice_fusion.2
  87.4 1.4 bitcast_dynamic-update-slice_fusion.2
  89.4 1.3 bitcast_dynamic-update-slice_fusion.2
  91.4 1.3 bitcast_dynamic-update-slice_fusion.2
  93.4 1.4 bitcast_dynamic-update-slice_fusion.2
  95.4 1.3 bitcast_dynamic-update-slice_fusion.2
  97.4 1.3 bitcast_dynamic-update-slice_fusion.2
  99.4 1.3 bitcast_dynamic-update-slice_fusion.2
  101.4 1.3 bitcast_dynamic-update-slice_fusion.2
  103.4 1.3 bitcast_dynamic-update-slice_fusion.2
  104.8 13.8 %all-gather.3.cloned.1.call-done = bf16[32,4,32768]{2,1,0:T(4,128)(2,1)} async-done(((bf16[1,4,32768]{2,1,0:T(4,128)(2,1)}), bf16[32,4,32768]{2,1,0:T(4,128)(2,1)}) %all-gather.3.cloned.1.call-update) | async-done | bytes 8388624 | tf_op jit(solution)/shard_map/all_gather | solution.py:57
  118.5 12.7 %reshape.131 = bf16[128,32768]{1,0:T(8,128)(2,1)} reshape(bf16[32,4,32768]{2,1,0:T(4,128)(2,1)} %all-gather.3.cloned.1.call-done) | data formatting | bytes 16777216
  131.2 4.6 %convolution_convert_fusion = bf16[24,32768]{1,0:T(8,128)(2,1)S(1)} fusion(bf16[128,32768]{1,0:T(8,128)(2,1)} %reshape.131, s32[24]{0:T(128)S(1)} %get-tuple-element.23), kind=kOutput, calls=%fused_computation.2 | convolution fusion | flops 202116096 | bytes 9961568 | tf_op jit(solution)/shard_map/dot_general | solution.py:61
  138.0 0.9 copy-done.3
  138.9 3.0 fusion.41
  142.0 1.8 fusion.42
  143.9 1.9 fusion.3
  145.8 1.8 convolution_convert_fusion.4
  148.1 1.0 reshape.135
  149.2 1.4 fusion.5
  150.5 6.3 %copy.35 = bf16[32,2,32768]{2,1,0:T(2,128)(2,1)} copy(bf16[32,2,32768]{2,0,1:T(8,128)(2,1)S(1)} %fusion.5) | data formatting | bytes 8388608 | tf_op jit(solution)/shard_map/dot_general | solution.py:113
  156.8 7.3 %all-to-all-start.1 = ((bf16[32,2,32768]{2,1,0:T(2,128)(2,1)}), bf16[32,2,32768]{2,1,0:T(2,128)(2,1)}, u32[]{:S(2)}, u32[]{:S(2)}) async-start(bf16[32,2,32768]{2,1,0:T(2,128)(2,1)} %copy.35), calls=%async_computation.1 | async-start | bytes 8388608 | tf_op jit(solution)/shard_map/all_to_all | solution.py:119
  165.0 2.6 reshape.109
  168.3 1.0 fusion.8
  169.3 1.3 dynamic-slice.4
  172.6 161.0 %all-reduce.4.cloned.1.call-done = f32[128,128]{1,0:T(8,128)} async-done(((f32[128,128]{1,0:T(8,128)}), f32[128,128]{1,0:T(8,128)}) %all-reduce.4.cloned.1.call-update) | async-done | bytes 65552
  333.6 1.3 constant_dynamic-slice_fusion.1
  334.8 7.3 %reshape.108 = bf16[64,32768]{1,0:T(8,128)(2,1)} reshape(bf16[32,2,32768]{2,1,0:T(2,128)(2,1)} %all-to-all-done.1) | data formatting | bytes 8388608 | tf_op jit(solution)/shard_map/reshape | solution.py:132
  342.1 3.6 %fusion.23 = f32[4,32768]{1,0:T(4,128)} fusion(bf16[64,32768]{1,0:T(8,128)(2,1)} %reshape.108, s32[64]{0:T(128)S(1)} %eq.115), kind=kOutput, calls=%fused_computation.45 | convolution fusion | flops 16777472 | bytes 4718848 | tf_op jit(solution)/shard_map/dot_general | solution.py:131
  (93 shorter events, 26.1 us)
Async XLA Ops:
  7.2 111.4 %all-gather.3.cloned.1.call-start = ((), (), s32[]{:S(2)}) async-start(), calls=%async_computation.2 | async-start | bytes 8650752 | tf_op jit(solution)/shard_map/all_gather | solution.py:57
  7.9 48.8 %collective-permute-start = (f32[1,32,1024]{2,1,0:T(8,128)}, f32[1,32,1024]{2,1,0:T(8,128)S(1)}, u32[]{:S(2)}, u32[]{:S(2)}) collective-permute-start(f32[1,32,1024]{2,1,0:T(8,128)} %param.6), channel_id=1, source_target_pairs={{32,0},{64,32},{96,64},{128,96},{160,128},{192,160},{224,192},{256... | collective-permute-start | bytes 393224 | tf_op jit(solution)/shard_map/ppermute | solution.py:12
  11.7 145.1 %all-to-all-start = ((s32[32,1,2]{2,1,0:T(1,128)}), s32[32,1,2]{2,1,0:T(1,128)S(1)}, u32[]{:S(2)}, u32[]{:S(2)}) async-start(s32[32,1,2]{2,1,0:T(1,128)} %bitcast.1), calls=%async_computation | async-start | bytes 32768 | tf_op jit(solution)/shard_map/all_to_all | solution.py:120
  25.3 7.5 %copy-start.5 = (s32[24]{0:T(128)S(1)}, s32[24]{0:T(128)}, u32[]{:S(2)}) copy-start(s32[24]{0:T(128)} %param.9) | copy-start | bytes 292
  45.3 11.4 %copy-start.4 = (f32[1,32,1024]{2,1,0:T(8,128)S(1)}, f32[1,32,1024]{2,1,0:T(8,128)}, u32[]{:S(2)}) copy-start(f32[1,32,1024]{2,1,0:T(8,128)} %param.6) | copy-start | bytes 393220
  137.4 1.6 copy-start.3
  142.0 1.9 copy-start.2
  145.8 1.8 copy-start
  156.8 7.4 %copy-start.1 = (bf16[768,1024]{1,0:T(8,128)(2,1)S(1)}, bf16[768,1024]{1,0:T(8,128)(2,1)}, u32[]{:S(2)}) copy-start(bf16[768,1024]{1,0:T(8,128)(2,1)} %copy-done) | copy-start | bytes 4718596
  156.8 178.0 %all-to-all-start.1 = ((bf16[32,2,32768]{2,1,0:T(2,128)(2,1)}), bf16[32,2,32768]{2,1,0:T(2,128)(2,1)}, u32[]{:S(2)}, u32[]{:S(2)}) async-start(bf16[32,2,32768]{2,1,0:T(2,128)(2,1)} %copy.35), calls=%async_computation.1 | async-start | bytes 8388608 | tf_op jit(solution)/shard_map/all_to_all | solution.py:119
  164.1 169.5 %all-reduce.4.cloned.1.call-start = ((), (), s32[]{:S(2)}) async-start(), calls=%async_computation.3 | async-start | bytes 131072
Sparse Core Ops, SparseCore 0:
  11.1 107.3 all-gather.2
  169.5 164.0 all-reduce.3
where the time goes:
time: 354 us; the launch traced here: 353 us
  waiting for transfers between devices  175 us (49%)
  local copies, waits for them, and re-layouts  108 us (31%)
  matrix products  21.8 us (6%)
  starting transfers between devices  20.9 us (6%)
  between operations  14.9 us (4%)
  other arithmetic  11.3 us (3%)
    unnamed x3, waiting for transfers between devices  162 us
    gather x72, local copies, waits for them, and re-layouts  47.9 us
    unnamed x16, local copies, waits for them, and re-layouts  17.1 us
    all_gather x1, waiting for transfers between devices, on_device(): gathered_rows = lax.all_gather(owned_blips, 'dom', axis=0, tiled=True)  13.8 us
    all_to_all x1, starting transfers between devices, on_device(): lax.all_to_all(asked_rows.reshape(domain_count, capacity), 'dom', split_a...  13.5 us
    convert_element_type x1, local copies, waits for them, and re-layouts, spline_tables(): plane_value.astype(jnp.bfloat16)  12.4 us
    convert_element_type x1, local copies, waits for them, and re-layouts, spline_tables(): plane_curve.astype(jnp.bfloat16)  11.4 us
    convert_element_type x1, other arithmetic, spline_tables(): plane_curve.astype(jnp.bfloat16)  7.53 us
  transfers between devices with their start and end apart: 5, of which 2 were waited for; matrix products, arithmetic and copies ran while one was open for 37% of the time, Pallas kernels for 0%

commit v1 on v0

--- a/solution.py
+++ b/solution.py
@@ -101,35 +101,32 @@
         jnp.float32
     )
     weighted = jnp.dot(intersection, select_full, precision=lax.Precision.HIGHEST)
-    part_hot = (
-        target[:, None] == jnp.arange(owned_count * lax.axis_size("dom"), dtype=jnp.int32)[None, :]
-    ).astype(jnp.float32)
-    hamilton = lax.psum_scatter(
-        jnp.dot(part_hot.T, weighted, precision=lax.Precision.HIGHEST),
-        "dom",
-        scatter_dimension=0,
-        tiled=True,
+    place_f32 = place_hot.astype(jnp.float32)
+    send_ham = jnp.concatenate(
+        [
+            jnp.dot(place_f32, weighted, precision=lax.Precision.HIGHEST),
+            asked_rows.astype(jnp.float32)[:, None],
+        ],
+        axis=1,
+    ).reshape(domain_count, capacity, group_size + 1)
+    got_ham = lax.all_to_all(send_ham, "dom", split_axis=0, concat_axis=0, tiled=True).reshape(
+        domain_count * capacity, group_size + 1
     )
+    got_rows = got_ham[:, group_size]
     send_grad = jnp.dot(
         place_low,
         gradient_piece.reshape(slot_count, cell_count),
         preferred_element_type=jnp.bfloat16,
     ).reshape(domain_count, capacity, cell_count)
-    got_grad, got_rows = (
-        lax.all_to_all(send_grad, "dom", split_axis=0, concat_axis=0, tiled=True),
-        lax.all_to_all(
-            asked_rows.reshape(domain_count, capacity),
-            "dom",
-            split_axis=0,
-            concat_axis=0,
-            tiled=True,
-        ),
+    got_grad = lax.all_to_all(send_grad, "dom", split_axis=0, concat_axis=0, tiled=True)
+    row_hot = got_rows[None, :] == jnp.arange(owned_count, dtype=jnp.float32)[:, None]
+    hamilton = jnp.dot(
+        row_hot.astype(jnp.float32), got_ham[:, :group_size], precision=lax.Precision.HIGHEST
     )
-    owner_pick = (
-        got_rows.reshape(-1)[None, :] == jnp.arange(owned_count, dtype=jnp.int32)[:, None]
-    ).astype(jnp.bfloat16)
     gradient = jnp.dot(
-        owner_pick, got_grad.reshape(-1, cell_count), preferred_element_type=jnp.float32
+        row_hot.astype(jnp.bfloat16),
+        got_grad.reshape(-1, cell_count),
+        preferred_element_type=jnp.float32,
     )
     return (gradient, hamilton)
 

time: 354 us -> 301 us (0.85)
  the two profiles are of different devices: /device:TPU:10 before, /device:TPU:8 now
where the time goes in v1:
time: 301 us; the launch traced here: 299 us
  waiting for transfers between devices  127 us (42%)
  local copies, waits for them, and re-layouts  104 us (35%)
  matrix products  27.1 us (9%)
  starting transfers between devices  15.4 us (5%)
  between operations  14.3 us (5%)
  other arithmetic  11.3 us (4%)
    all_to_all x1, waiting for transfers between devices, on_device(): lax.all_to_all(send_grad, 'dom', split_axis=0, concat_axis=0, tiled=True)  95 us
    gather x72, local copies, waits for them, and re-layouts  45.5 us
    all_gather x1, waiting for transfers between devices, on_device(): gathered_rows = lax.all_gather(owned_blips, 'dom', axis=0, tiled=True)  31.4 us
    unnamed x12, local copies, waits for them, and re-layouts  14.5 us
    convert_element_type x1, local copies, waits for them, and re-layouts, spline_tables(): plane_value.astype(jnp.bfloat16)  12.4 us
    convert_element_type x1, local copies, waits for them, and re-layouts, spline_tables(): plane_curve.astype(jnp.bfloat16)  11.4 us
    all_to_all x1, starting transfers between devices, on_device(): lax.all_to_all(send_grad, 'dom', split_axis=0, concat_axis=0, tiled=True)  9.69 us
    convert_element_type x1, other arithmetic, spline_tables(): plane_curve.astype(jnp.bfloat16)  7.56 us
  transfers between devices with their start and end apart: 4, of which 2 were waited for; matrix products, arithmetic and copies ran while one was open for 31% of the time, Pallas kernels for 0%

profile of v1, /device:TPU:8, one launch (start us, length us, event | category | flops | bytes accessed | tf_op | source)
XLA Modules:
  0.0 299.2 jit_solution(602557687519509434)
XLA Ops:
  8.9 0.8 select_reduce_fusion.1
  11.2 7.6 %fusion.1 = (bf16[32,32,32,32]{3,2,1,0:T(8,128)(2,1)}, bf16[32,32,32,32]{3,2,1,0:T(8,128)(2,1)}) fusion(f32[32,32]{1,0:T(8,128)S(1)} %copy.43, f32[32,32]{1,0:T(8,128)S(1)} %copy.40), kind=kLoop, calls=%fused_computation.6 | loop fusion | flops 6291456 | bytes 4202496 | tf_op jit(solution)/shard_map/convert_element_type | solution.py:32
  18.7 12.4 %convert_element_type.92 = bf16[1024,1024]{1,0:T(8,128)(2,1)} reshape(bf16[32,32,32,32]{3,2,1,0:T(8,128)(2,1)} %get-tuple-element.21) | data formatting | bytes 4194304 | tf_op jit(solution)/shard_map/convert_element_type | solution.py:31
  31.1 11.4 %convert_element_type.99 = bf16[1024,1024]{1,0:T(8,128)(2,1)S(1)} reshape(bf16[32,32,32,32]{3,2,1,0:T(8,128)(2,1)} %get-tuple-element.20) | data formatting | bytes 4194304 | tf_op jit(solution)/shard_map/convert_element_type | solution.py:32
  42.8 45.6 %while.1 = (s32[]{:T(128)}, f32[64,1024]{1,0:T(8,128)S(1)}, s32[24,2]{0,1:T(2,128)S(1)}, f32[24,32,1024]{2,1,0:T(8,128)}, s32[]{:T(128)}) while((s32[]{:T(128)}, f32[64,1024]{1,0:T(8,128)S(1)}, s32[24,2]{0,1:T(2,128)S(1)}, f32[24,32,1024]{2,1,0:T(8,128)}, s32[]{:T(128)}) %tuple.24), condition=%wide.while_cond, body=%wide.while_body.sunk | while | flops 2 | bytes 263257 | solution.py:68
  43.4 1.3 bitcast_dynamic-update-slice_fusion.2
  45.3 1.3 bitcast_dynamic-update-slice_fusion.2
  47.2 1.3 bitcast_dynamic-update-slice_fusion.2
  49.1 1.3 bitcast_dynamic-update-slice_fusion.2
  51.0 1.3 bitcast_dynamic-update-slice_fusion.2
  52.9 1.3 bitcast_dynamic-update-slice_fusion.2
  54.8 1.3 bitcast_dynamic-update-slice_fusion.2
  56.7 1.3 bitcast_dynamic-update-slice_fusion.2
  58.5 1.3 bitcast_dynamic-update-slice_fusion.2
  60.5 1.3 bitcast_dynamic-update-slice_fusion.2
  62.3 1.3 bitcast_dynamic-update-slice_fusion.2
  64.2 1.3 bitcast_dynamic-update-slice_fusion.2
  66.1 1.3 bitcast_dynamic-update-slice_fusion.2
  68.0 1.3 bitcast_dynamic-update-slice_fusion.2
  69.9 1.3 bitcast_dynamic-update-slice_fusion.2
  71.8 1.3 bitcast_dynamic-update-slice_fusion.2
  73.7 1.3 bitcast_dynamic-update-slice_fusion.2
  75.6 1.3 bitcast_dynamic-update-slice_fusion.2
  77.5 1.3 bitcast_dynamic-update-slice_fusion.2
  79.4 1.3 bitcast_dynamic-update-slice_fusion.2
  81.3 1.3 bitcast_dynamic-update-slice_fusion.2
  83.3 1.3 bitcast_dynamic-update-slice_fusion.2
  85.1 1.3 bitcast_dynamic-update-slice_fusion.2
  87.0 1.3 bitcast_dynamic-update-slice_fusion.2
  88.4 31.4 %all-gather.3.cloned.1.call-done = bf16[32,4,32768]{2,1,0:T(4,128)(2,1)} async-done(((bf16[1,4,32768]{2,1,0:T(4,128)(2,1)}), bf16[32,4,32768]{2,1,0:T(4,128)(2,1)}) %all-gather.3.cloned.1.call-update) | async-done | bytes 8388624 | tf_op jit(solution)/shard_map/all_gather | solution.py:57
  119.8 12.7 %reshape.138 = bf16[128,32768]{1,0:T(8,128)(2,1)} reshape(bf16[32,4,32768]{2,1,0:T(4,128)(2,1)} %all-gather.3.cloned.1.call-done) | data formatting | bytes 16777216
  132.4 4.6 %convolution_convert_fusion = bf16[24,32768]{1,0:T(8,128)(2,1)S(1)} fusion(bf16[128,32768]{1,0:T(8,128)(2,1)} %reshape.138, s32[24]{0:T(128)S(1)} %get-tuple-element.23), kind=kOutput, calls=%fused_computation.2 | convolution fusion | flops 202116096 | bytes 9961568 | tf_op jit(solution)/shard_map/dot_general | solution.py:61
  137.1 0.9 copy.51
  139.3 0.9 copy-done.2
  140.2 3.0 fusion.44
  143.2 1.8 fusion.45
  145.1 3.1 %fusion.3 = bf16[768,1024]{1,0:T(8,128)(2,1)} fusion(f32[768,1024]{1,0:T(8,128)S(1)} %get-tuple-element.25, f32[24,32,1024]{2,1,0:T(8,128)S(1)} %copy-done.1, f32[768,1024]{1,0:T(8,128)S(1)} %fusion.45, bf16[768,1024]{1,0:T(8,128)(2,1)S(1)} %bitcast.71, bf16[1024,1024]{1,0:T(8,128)(2,1)S(1)} %convert_element_type.99), kind=kOutput, calls=%fused_computation.9 | convolution fusion | flops 1614544896 | bytes 14680064 | tf_op jit(solution)/shard_map/dot_general | solution.py:82
  148.1 2.7 reshape.113
  150.8 4.5 %convolution_convert_fusion.4 = bf16[768,1024]{1,0:T(8,128)(2,1)} fusion(bf16[768,1024]{1,0:T(8,128)(2,1)S(1)} %copy-done, bf16[1024,1024]{1,0:T(8,128)(2,1)} %convert_element_type.92), kind=kOutput, calls=%fused_computation.13 | convolution fusion | flops 1611399168 | bytes 5242880 | tf_op jit(solution)/shard_map/dot_general | solution.py:85
  155.4 2.6 reshape.110
  159.7 5.7 %all-to-all-start = ((f32[32,2,129]{2,1,0:T(2,128)}), f32[32,2,129]{2,1,0:T(2,128)S(1)}, u32[]{:S(2)}, u32[]{:S(2)}) async-start(f32[32,2,129]{2,1,0:T(2,128)} %pad_maximum_fusion.1), calls=%async_computation | async-start | bytes 131072 | tf_op jit(solution)/shard_map/all_to_all | solution.py:112
  165.4 2.0 fusion.4
  168.2 1.4 fusion.7
  169.5 6.3 %copy.46 = bf16[32,2,32768]{2,1,0:T(2,128)(2,1)} copy(bf16[32,2,32768]{2,0,1:T(8,128)(2,1)S(1)} %fusion.7) | data formatting | bytes 8388608 | tf_op jit(solution)/shard_map/dot_general | solution.py:116
  175.8 9.7 %all-to-all-start.1 = ((bf16[32,2,32768]{2,1,0:T(2,128)(2,1)}), bf16[32,2,32768]{2,1,0:T(2,128)(2,1)}, u32[]{:S(2)}, u32[]{:S(2)}) async-start(bf16[32,2,32768]{2,1,0:T(2,128)(2,1)} %copy.46), calls=%async_computation.1 | async-start | bytes 8388608 | tf_op jit(solution)/shard_map/all_to_all | solution.py:121
  186.4 95.0 %all-to-all-done.1 = bf16[32,2,32768]{2,1,0:T(2,128)(2,1)} async-done(((bf16[32,2,32768]{2,1,0:T(2,128)(2,1)}), bf16[32,2,32768]{2,1,0:T(2,128)(2,1)}, u32[]{:S(2)}, u32[]{:S(2)}) %all-to-all-start.1) | async-done | bytes 4194336 | tf_op jit(solution)/shard_map/all_to_all | solution.py:121
  281.4 7.3 %reshape.117 = bf16[64,32768]{1,0:T(8,128)(2,1)} reshape(bf16[32,2,32768]{2,1,0:T(2,128)(2,1)} %all-to-all-done.1) | data formatting | bytes 8388608 | tf_op jit(solution)/shard_map/reshape | solution.py:128
  288.7 3.6 %fusion.25 = f32[4,32768]{1,0:T(4,128)} fusion(bf16[64,32768]{1,0:T(8,128)(2,1)} %reshape.117, f32[64]{0:T(128)S(1)} %slice_reduce_fusion), kind=kOutput, calls=%fused_computation.49 | convolution fusion | flops 16777472 | bytes 4718848 | tf_op jit(solution)/shard_map/dot_general | solution.py:126
  (87 shorter events, 22.2 us)
Async XLA Ops:
  7.2 112.6 %all-gather.3.cloned.1.call-start = ((), (), s32[]{:S(2)}) async-start(), calls=%async_computation.2 | async-start | bytes 8650752 | tf_op jit(solution)/shard_map/all_gather | solution.py:57
  7.9 34.8 %collective-permute-start = (f32[1,32,1024]{2,1,0:T(8,128)}, f32[1,32,1024]{2,1,0:T(8,128)S(1)}, u32[]{:S(2)}, u32[]{:S(2)}) collective-permute-start(f32[1,32,1024]{2,1,0:T(8,128)} %param.6), channel_id=1, source_target_pairs={{32,0},{64,32},{96,64},{128,96},{160,128},{192,160},{224,192},{256... | collective-permute-start | bytes 393224 | tf_op jit(solution)/shard_map/ppermute | solution.py:12
  11.1 7.6 %copy-start.4 = (s32[24]{0:T(128)S(1)}, s32[24]{0:T(128)}, u32[]{:S(2)}) copy-start(s32[24]{0:T(128)} %param.9) | copy-start | bytes 292
  31.1 11.6 %copy-start.3 = (f32[1,32,1024]{2,1,0:T(8,128)S(1)}, f32[1,32,1024]{2,1,0:T(8,128)}, u32[]{:S(2)}) copy-start(f32[1,32,1024]{2,1,0:T(8,128)} %param.6) | copy-start | bytes 393220
  138.6 1.6 copy-start.2
  143.2 1.9 copy-start.1
  148.1 2.7 copy-start
  159.7 16.1 %all-to-all-start = ((f32[32,2,129]{2,1,0:T(2,128)}), f32[32,2,129]{2,1,0:T(2,128)S(1)}, u32[]{:S(2)}, u32[]{:S(2)}) async-start(f32[32,2,129]{2,1,0:T(2,128)} %pad_maximum_fusion.1), calls=%async_computation | async-start | bytes 131072 | tf_op jit(solution)/shard_map/all_to_all | solution.py:112
  175.8 105.6 %all-to-all-start.1 = ((bf16[32,2,32768]{2,1,0:T(2,128)(2,1)}), bf16[32,2,32768]{2,1,0:T(2,128)(2,1)}, u32[]{:S(2)}, u32[]{:S(2)}) async-start(bf16[32,2,32768]{2,1,0:T(2,128)(2,1)} %copy.46), calls=%async_computation.1 | async-start | bytes 8388608 | tf_op jit(solution)/shard_map/all_to_all | solution.py:121
Sparse Core Ops, SparseCore 0:
  11.1 108.5 all-gather.2

commit v2 on v1

--- a/solution.py
+++ b/solution.py
@@ -53,14 +53,9 @@
     asked_rows = jnp.sum(jnp.where(place_hot, slot_row[None, :], 0), axis=1) + owned_count * (
         1 - jnp.sum(place_hot.astype(jnp.int32), axis=1)
     )
-    place_low = place_hot.astype(jnp.bfloat16)
-    gathered_rows = lax.all_gather(owned_blips, "dom", axis=0, tiled=True)
-    chosen = (
-        target[:, None] == jnp.arange(gathered_rows.shape[0], dtype=jnp.int32)[None, :]
-    ).astype(jnp.bfloat16)
-    slot_blips = jnp.dot(chosen, gathered_rows, preferred_element_type=jnp.float32).astype(
-        jnp.bfloat16
-    )
+    blocks = owned_blips.reshape(owned_count, NB, plane_cells)
+    gathered_blocks = lax.all_gather(blocks, "dom", axis=0, tiled=True)
+    slot_blips = jnp.take(gathered_blocks, target, axis=0, mode="clip")
     upper_cells = passed_along(potential, "grp", -1)
     extended = jnp.concatenate([potential[0], upper_cells[0]], axis=0)
 
@@ -68,7 +63,7 @@
         return lax.dynamic_slice_in_dim(extended, first_row, NB, 0)
 
     window = jax.vmap(cut_window)(slot_offset)
-    layered = slot_blips.reshape(slot_count, NB, plane_cells)
+    layered = slot_blips
     y_value = jnp.einsum("ya,sab->syb", spline, layered, preferred_element_type=jnp.float32).astype(
         jnp.bfloat16
     )
@@ -113,21 +108,22 @@
         domain_count * capacity, group_size + 1
     )
     got_rows = got_ham[:, group_size]
-    send_grad = jnp.dot(
-        place_low,
-        gradient_piece.reshape(slot_count, cell_count),
-        preferred_element_type=jnp.bfloat16,
-    ).reshape(domain_count, capacity, cell_count)
-    got_grad = lax.all_to_all(send_grad, "dom", split_axis=0, concat_axis=0, tiled=True)
+    piece_of_place = jnp.sum(
+        jnp.where(place_hot, jnp.arange(slot_count, dtype=jnp.int32)[None, :], 0), axis=1
+    )
+    send_grad = jnp.take(
+        gradient_piece.reshape(slot_count, NB, plane_cells), piece_of_place, axis=0, mode="clip"
+    ).reshape(domain_count, capacity * NB, plane_cells)
+    got_grad = lax.all_to_all(send_grad, "dom", split_axis=0, concat_axis=0, tiled=True).reshape(
+        domain_count * capacity, NB, plane_cells
+    )
     row_hot = got_rows[None, :] == jnp.arange(owned_count, dtype=jnp.float32)[:, None]
     hamilton = jnp.dot(
         row_hot.astype(jnp.float32), got_ham[:, :group_size], precision=lax.Precision.HIGHEST
     )
-    gradient = jnp.dot(
-        row_hot.astype(jnp.bfloat16),
-        got_grad.reshape(-1, cell_count),
-        preferred_element_type=jnp.float32,
-    )
+    gradient = jnp.einsum(
+        "rs,syc->ryc", row_hot.astype(jnp.bfloat16), got_grad, preferred_element_type=jnp.float32
+    ).reshape(owned_count, cell_count)
     return (gradient, hamilton)
 
 

time: 301 us -> 274 us (0.910)
  local copies, waits for them, and re-layouts: 104 us -> 89.2 us
  matrix products: 27.1 us -> 17.8 us
  starting transfers between devices: 15.4 us -> 10.4 us
    dot_general x3 -> x1, matrix products: 9.61 us -> 1.45 us  [on_device(): jnp.einsum('rs,syc->ryc', row_hot.astype(jnp.bfloat16), got_grad, preferr...]
    reshape x2 -> x0, local copies, waits for them, and re-layouts: 8.05 us -> none  [the longest x1 7.27 us: on_device(): got_grad.reshape(-1, cell_count)]
    gather x72 -> x74, local copies, waits for them, and re-layouts: 45.5 us -> 52.3 us
    unnamed x12 -> x10, local copies, waits for them, and re-layouts: 14.5 us -> 8.02 us
    dot_general x1 -> x0, local copies, waits for them, and re-layouts: 6.28 us -> none  [on_device(): jnp.dot(place_low, gradient_piece.reshape(slot_count, cell_count), prefer...]
    all_to_all x1, waiting for transfers between devices: 0.01 us -> 5.35 us  [on_device(): lax.all_to_all(send_ham, 'dom', split_axis=0, concat_axis=0, tiled=True)]
    all_to_all x1, starting transfers between devices: 9.69 us -> 4.85 us  [on_device(): lax.all_to_all(send_grad, 'dom', split_axis=0, concat_axis=0, tiled=True)]
  transfers between devices with their start and end apart: 4 -> 4, of which waited for: 2 -> 3; matrix products, arithmetic and copies ran while one was open for 31% -> 32% of each run, Pallas kernels for 0% -> 0%
where the time goes in v2:
time: 274 us; the launch traced here: 273 us
  waiting for transfers between devices  129 us (47%)
  local copies, waits for them, and re-layouts  89.2 us (33%)
  matrix products  17.8 us (6%)
  between operations  14.2 us (5%)
  other arithmetic  12 us (4%)
  starting transfers between devices  10.4 us (4%)
    all_to_all x1, waiting for transfers between devices, on_device(): lax.all_to_all(send_grad, 'dom', split_axis=0, concat_axis=0, tiled=True)  94.8 us
    gather x72, local copies, waits for them, and re-layouts  45.4 us
    all_gather x1, waiting for transfers between devices, on_device(): gathered_blocks = lax.all_gather(blocks, 'dom', axis=0, tiled=True)  29.2 us
    convert_element_type x1, local copies, waits for them, and re-layouts, spline_tables(): plane_curve.astype(jnp.bfloat16)  12.5 us
    convert_element_type x1, local copies, waits for them, and re-layouts, spline_tables(): plane_value.astype(jnp.bfloat16)  12.4 us
    unnamed x10, local copies, waits for them, and re-layouts  8.02 us
    convert_element_type x1, other arithmetic, spline_tables(): plane_curve.astype(jnp.bfloat16)  7.59 us
    all_to_all x1, starting transfers between devices, on_device(): lax.all_to_all(send_ham, 'dom', split_axis=0, concat_axis=0, tiled=True)  5.54 us
  transfers between devices with their start and end apart: 4, of which 3 were waited for; matrix products, arithmetic and copies ran while one was open for 32% of the time, Pallas kernels for 0%

profile of v2, /device:TPU:8, one launch (start us, length us, event | category | flops | bytes accessed | tf_op | source)
XLA Modules:
  0.0 273.0 jit_solution(11746492043986911821)
XLA Ops:
  7.2 1.7 copy.50
  9.9 0.8 select_reduce_fusion.2
  11.5 0.7 convert_reduce_fusion
  12.9 7.6 %fusion.1 = (bf16[32,32,32,32]{3,2,1,0:T(8,128)(2,1)}, bf16[32,32,32,32]{3,2,1,0:T(8,128)(2,1)}) fusion(f32[32,32]{1,0:T(8,128)S(1)} %copy.40, f32[32,32]{1,0:T(8,128)S(1)} %copy.37), kind=kLoop, calls=%fused_computation.7 | loop fusion | flops 6291456 | bytes 4202496 | tf_op jit(solution)/shard_map/convert_element_type | solution.py:32
  20.5 12.4 %convert_element_type.86 = bf16[1024,1024]{1,0:T(8,128)(2,1)} reshape(bf16[32,32,32,32]{3,2,1,0:T(8,128)(2,1)} %get-tuple-element.22) | data formatting | bytes 4194304 | tf_op jit(solution)/shard_map/convert_element_type | solution.py:31
  32.9 12.5 %convert_element_type.93 = bf16[1024,1024]{1,0:T(8,128)(2,1)} reshape(bf16[32,32,32,32]{3,2,1,0:T(8,128)(2,1)} %get-tuple-element.21) | data formatting | bytes 4194304 | tf_op jit(solution)/shard_map/convert_element_type | solution.py:32
  45.6 45.5 %while.1 = (s32[]{:T(128)}, f32[64,1024]{1,0:T(8,128)S(1)}, s32[24,2]{0,1:T(2,128)S(1)}, f32[24,32,1024]{2,1,0:T(8,128)}, s32[]{:T(128)}) while((s32[]{:T(128)}, f32[64,1024]{1,0:T(8,128)S(1)}, s32[24,2]{0,1:T(2,128)S(1)}, f32[24,32,1024]{2,1,0:T(8,128)}, s32[]{:T(128)}) %tuple.25), condition=%wide.while_cond, body=%wide.while_body.sunk | while | flops 2 | bytes 263257 | solution.py:63
  46.2 1.3 bitcast_dynamic-update-slice_fusion.2
  48.1 1.3 bitcast_dynamic-update-slice_fusion.2
  50.0 1.3 bitcast_dynamic-update-slice_fusion.2
  51.9 1.3 bitcast_dynamic-update-slice_fusion.2
  53.8 1.3 bitcast_dynamic-update-slice_fusion.2
  55.7 1.3 bitcast_dynamic-update-slice_fusion.2
  57.6 1.3 bitcast_dynamic-update-slice_fusion.2
  59.5 1.3 bitcast_dynamic-update-slice_fusion.2
  61.4 1.3 bitcast_dynamic-update-slice_fusion.2
  63.3 1.3 bitcast_dynamic-update-slice_fusion.2
  65.2 1.3 bitcast_dynamic-update-slice_fusion.2
  67.1 1.3 bitcast_dynamic-update-slice_fusion.2
  69.0 1.3 bitcast_dynamic-update-slice_fusion.2
  70.9 1.3 bitcast_dynamic-update-slice_fusion.2
  72.8 1.3 bitcast_dynamic-update-slice_fusion.2
  74.7 1.3 bitcast_dynamic-update-slice_fusion.2
  76.6 1.3 bitcast_dynamic-update-slice_fusion.2
  78.5 1.3 bitcast_dynamic-update-slice_fusion.2
  80.4 1.3 bitcast_dynamic-update-slice_fusion.2
  82.3 1.3 bitcast_dynamic-update-slice_fusion.2
  84.1 1.3 bitcast_dynamic-update-slice_fusion.2
  86.1 1.3 bitcast_dynamic-update-slice_fusion.2
  88.0 1.3 bitcast_dynamic-update-slice_fusion.2
  89.8 1.3 bitcast_dynamic-update-slice_fusion.2
  91.1 29.2 %all-gather.2.cloned.1.call-done = bf16[128,32,1024]{2,1,0:T(8,128)(2,1)} async-done(((bf16[4,32,1024]{2,1,0:T(8,128)(2,1)}), bf16[128,32,1024]{2,1,0:T(8,128)(2,1)}) %all-gather.2.cloned.1.call-update) | async-done | bytes 8388624 | tf_op jit(solution)/shard_map/all_gather | solution.py:57
  120.3 4.0 %gather_fusion = bf16[24,32,1024]{2,1,0:T(8,128)(2,1)S(1)} fusion(bf16[128,32,1024]{2,1,0:T(8,128)(2,1)} %all-gather.2.cloned.1.call-done, s32[1024]{0:T(1024)S(1)} %pad_clamp_fusion.1), kind=kCustom, calls=%fused_computation | custom fusion | bytes 3145824 | tf_op jit(solution)/shard_map/jit(_take)/gather | solution.py:58
  125.6 0.9 copy-done.2
  126.6 3.0 %fusion.39 = (bf16[768,1024]{1,0:T(8,128)(2,1)}, f32[768,1024]{1,0:T(8,128)S(1)}) fusion(bf16[768,1024]{1,0:T(8,128)(2,1)S(1)} %bitcast.77, bf16[1024,1024]{1,0:T(8,128)(2,1)S(1)} %copy-done.2), kind=kOutput, calls=%fused_computation.71 | convolution fusion | flops 1611399168 | bytes 8388608 | tf_op jit(solution)/shard_map/dot_general | solution.py:74
  129.5 1.8 fusion.40
  132.1 1.9 fusion.3
  134.0 0.8 reshape.96
  134.8 4.6 %convolution_convert_fusion.3 = bf16[768,1024]{1,0:T(8,128)(2,1)} fusion(bf16[768,1024]{1,0:T(8,128)(2,1)S(1)} %fusion.3, bf16[1024,1024]{1,0:T(8,128)(2,1)} %convert_element_type.86), kind=kOutput, calls=%fused_computation.14 | convolution fusion | flops 1611399168 | bytes 5242880 | tf_op jit(solution)/shard_map/dot_general | solution.py:80
  139.3 2.8 %reshape.93 = bf16[24,32768]{1,0:T(8,128)(2,1)S(1)} reshape(bf16[768,1024]{1,0:T(8,128)(2,1)} %get-tuple-element.25) | data formatting | bytes 3145728 | tf_op jit(solution)/shard_map/reshape | solution.py:90
  143.9 5.5 %all-to-all-start = ((f32[32,2,129]{2,1,0:T(2,128)}), f32[32,2,129]{2,1,0:T(2,128)S(1)}, u32[]{:S(2)}, u32[]{:S(2)}) async-start(f32[32,2,129]{2,1,0:T(2,128)} %pad_maximum_fusion.1), calls=%async_computation | async-start | bytes 131072 | tf_op jit(solution)/shard_map/all_to_all | solution.py:107
  149.4 2.0 fusion.4
  151.4 2.8 %gather_fusion.1 = bf16[64,32,1024]{2,1,0:T(8,128)(2,1)} fusion(bf16[24,32,1024]{2,1,0:T(8,128)(2,1)S(1)} %fusion.4, s32[1024]{0:T(1024)S(1)} %pad_clamp_fusion), kind=kCustom, calls=%fused_computation.1 | custom fusion | bytes 8388864 | tf_op jit(solution)/shard_map/jit(_take)/gather | solution.py:114
  154.2 5.4 %all-to-all-done = f32[32,2,129]{2,1,0:T(2,128)S(1)} async-done(((f32[32,2,129]{2,1,0:T(2,128)}), f32[32,2,129]{2,1,0:T(2,128)S(1)}, u32[]{:S(2)}, u32[]{:S(2)}) %all-to-all-start) | async-done | bytes 33056 | tf_op jit(solution)/shard_map/all_to_all | solution.py:107
  159.5 4.8 %all-to-all-start.1 = ((bf16[32,64,1024]{2,1,0:T(8,128)(2,1)}), bf16[32,64,1024]{2,1,0:T(8,128)(2,1)}, u32[]{:S(2)}, u32[]{:S(2)}) async-start(bf16[32,64,1024]{2,1,0:T(8,128)(2,1)} %bitcast.75), calls=%async_computation.1 | async-start | bytes 8388608 | tf_op jit(solution)/shard_map/all_to_all | solution.py:117
  165.3 94.8 %all-to-all-done.1 = bf16[32,64,1024]{2,1,0:T(8,128)(2,1)} async-done(((bf16[32,64,1024]{2,1,0:T(8,128)(2,1)}), bf16[32,64,1024]{2,1,0:T(8,128)(2,1)}, u32[]{:S(2)}, u32[]{:S(2)}) %all-to-all-start.1) | async-done | bytes 4194336 | tf_op jit(solution)/shard_map/all_to_all | solution.py:117
  260.1 4.6 %copy.48 = bf16[8,8,32,1024]{3,1,2,0:T(8,128)(2,1)S(1)} copy(bf16[8,8,32,1024]{3,2,1,0:T(8,128)(2,1)} %bitcast.30) | data formatting | bytes 8388608
  264.7 1.5 fusion.20
  (83 shorter events, 22.1 us)
Async XLA Ops:
  7.2 113.1 %all-gather.2.cloned.1.call-start = ((), (), s32[]{:S(2)}) async-start(), calls=%async_computation.2 | async-start | bytes 8650752 | tf_op jit(solution)/shard_map/all_gather | solution.py:57
  9.0 36.6 %collective-permute-start = (f32[1,32,1024]{2,1,0:T(8,128)}, f32[1,32,1024]{2,1,0:T(8,128)S(1)}, u32[]{:S(2)}, u32[]{:S(2)}) collective-permute-start(f32[1,32,1024]{2,1,0:T(8,128)} %param.6), channel_id=1, source_target_pairs={{32,0},{64,32},{96,64},{128,96},{160,128},{192,160},{224,192},{256... | collective-permute-start | bytes 393224 | tf_op jit(solution)/shard_map/ppermute | solution.py:12
  32.9 12.7 %copy-start.3 = (f32[1,32,1024]{2,1,0:T(8,128)S(1)}, f32[1,32,1024]{2,1,0:T(8,128)}, u32[]{:S(2)}) copy-start(f32[1,32,1024]{2,1,0:T(8,128)} %param.6) | copy-start | bytes 393220
  125.0 1.6 copy-start.2
  129.5 1.8 copy-start
  129.5 2.5 copy-start.1
  143.9 15.6 %all-to-all-start = ((f32[32,2,129]{2,1,0:T(2,128)}), f32[32,2,129]{2,1,0:T(2,128)S(1)}, u32[]{:S(2)}, u32[]{:S(2)}) async-start(f32[32,2,129]{2,1,0:T(2,128)} %pad_maximum_fusion.1), calls=%async_computation | async-start | bytes 131072 | tf_op jit(solution)/shard_map/all_to_all | solution.py:107
  159.5 100.5 %all-to-all-start.1 = ((bf16[32,64,1024]{2,1,0:T(8,128)(2,1)}), bf16[32,64,1024]{2,1,0:T(8,128)(2,1)}, u32[]{:S(2)}, u32[]{:S(2)}) async-start(bf16[32,64,1024]{2,1,0:T(8,128)(2,1)} %bitcast.75), calls=%async_computation.1 | async-start | bytes 8388608 | tf_op jit(solution)/shard_map/all_to_all | solution.py:117
Sparse Core Ops, SparseCore 0:
  11.7 108.5 all-gather.1

commit v3 on v2

--- a/solution.py
+++ b/solution.py
@@ -2,6 +2,7 @@
 import jax.numpy as jnp
 from jax import lax
 from jax.sharding import PartitionSpec as P
+
 
 NB = 32
 
@@ -54,8 +55,12 @@
         1 - jnp.sum(place_hot.astype(jnp.int32), axis=1)
     )
     blocks = owned_blips.reshape(owned_count, NB, plane_cells)
-    gathered_blocks = lax.all_gather(blocks, "dom", axis=0, tiled=True)
-    slot_blips = jnp.take(gathered_blocks, target, axis=0, mode="clip")
+    half = plane_cells // 2
+    early = half - 4 * NB
+    gathered_a = lax.all_gather(blocks[:, :, :half], "dom", axis=0, tiled=True)
+    gathered_b = lax.all_gather(blocks[:, :, half:], "dom", axis=0, tiled=True)
+    blips_a = jnp.take(gathered_a, target, axis=0, mode="clip")
+    blips_b = jnp.take(gathered_b, target, axis=0, mode="clip")
     upper_cells = passed_along(potential, "grp", -1)
     extended = jnp.concatenate([potential[0], upper_cells[0]], axis=0)
 
@@ -63,34 +68,75 @@
         return lax.dynamic_slice_in_dim(extended, first_row, NB, 0)
 
     window = jax.vmap(cut_window)(slot_offset)
-    layered = slot_blips
-    y_value = jnp.einsum("ya,sab->syb", spline, layered, preferred_element_type=jnp.float32).astype(
-        jnp.bfloat16
+
+    def y_pass(table, layered):
+        return jnp.einsum(
+            "ya,sab->syb", table, layered, preferred_element_type=jnp.float32
+        ).astype(jnp.bfloat16)
+
+    def flat(block):
+        return block.reshape(-1, block.shape[-1])
+
+    def plane_terms(y_value, y_curve, value_cols, curve_cols, window_cols):
+        values_grid = jnp.dot(flat(y_value), value_cols, preferred_element_type=jnp.float32)
+        laplace = jnp.dot(flat(y_curve), value_cols, preferred_element_type=jnp.float32) + jnp.dot(
+            flat(y_value), curve_cols, preferred_element_type=jnp.float32
+        )
+        applied = (-0.5 * laplace + flat(window_cols) * values_grid).astype(jnp.bfloat16)
+        return applied, values_grid.astype(jnp.bfloat16)
+
+    def gradient_of(applied_rows, value_cols):
+        back_plane = jnp.dot(applied_rows, value_cols, preferred_element_type=jnp.float32).astype(
+            jnp.bfloat16
+        )
+        return jnp.einsum(
+            "ay,sab->syb",
+            spline,
+            back_plane.reshape(slot_count, NB, -1),
+            preferred_element_type=jnp.float32,
+        ).astype(jnp.bfloat16)
+
+    piece_of_place = jnp.sum(
+        jnp.where(place_hot, jnp.arange(slot_count, dtype=jnp.int32)[None, :], 0), axis=1
     )
-    y_curve = jnp.einsum("ya,sab->syb", second, layered, preferred_element_type=jnp.float32).astype(
-        jnp.bfloat16
+
+    def send_gradient(gradient_piece):
+        send = jnp.take(gradient_piece, piece_of_place, axis=0, mode="clip")
+        send = send.reshape(domain_count, capacity * NB, send.shape[-1])
+        got = lax.all_to_all(send, "dom", split_axis=0, concat_axis=0, tiled=True)
+        return got.reshape(domain_count * capacity, NB, -1)
+
+    y_value_a = y_pass(spline, blips_a)
+    y_curve_a = y_pass(second, blips_a)
+    applied_a, values_low_a = plane_terms(
+        y_value_a,
+        y_curve_a,
+        plane_value[:half, :half],
+        plane_curve[:half, :half],
+        window[:, :, :half],
     )
-    flat_value = y_value.reshape(-1, plane_cells)
-    values_grid = jnp.dot(flat_value, plane_value, preferred_element_type=jnp.float32)
-    laplace = jnp.dot(
-        y_curve.reshape(-1, plane_cells), plane_value, preferred_element_type=jnp.float32
-    ) + jnp.dot(flat_value, plane_curve, preferred_element_type=jnp.float32)
-    applied = (-0.5 * laplace + window.reshape(-1, plane_cells) * values_grid).astype(jnp.bfloat16)
-    values_low = values_grid.astype(jnp.bfloat16)
-    back_plane = jnp.dot(applied, plane_value, preferred_element_type=jnp.float32).astype(
-        jnp.bfloat16
+    gradient_a = gradient_of(applied_a, plane_value[:half, :early])
+    got_grad_a = send_gradient(gradient_a)
+    y_value = jnp.concatenate([y_value_a, y_pass(spline, blips_b)], axis=2)
+    y_curve = jnp.concatenate([y_curve_a, y_pass(second, blips_b)], axis=2)
+    applied_b, values_low_b = plane_terms(
+        y_value, y_curve, plane_value[:, early:], plane_curve[:, early:], window[:, :, early:]
     )
-    gradient_piece = jnp.einsum(
-        "ay,sab->syb",
-        spline,
-        back_plane.reshape(slot_count, NB, plane_cells),
-        preferred_element_type=jnp.float32,
-    ).astype(jnp.bfloat16)
-    intersection = lax.dot_general(
-        values_low.reshape(slot_count, cell_count),
-        applied.reshape(slot_count, cell_count),
-        (((1,), (1,)), ((), ())),
-        preferred_element_type=jnp.float32,
+    applied_rows = jnp.concatenate([applied_a[:, :early], applied_b], axis=1)
+    gradient_b = gradient_of(applied_rows, plane_value[:, early:])
+    got_grad_b = send_gradient(gradient_b)
+
+
+    def overlap(values_low, applied):
+        return lax.dot_general(
+            values_low.reshape(slot_count, NB, -1),
+            applied.reshape(slot_count, NB, -1),
+            (((1, 2), (1, 2)), ((), ())),
+            preferred_element_type=jnp.float32,
+        )
+
+    intersection = (
+        overlap(values_low_a[:, :early], applied_a[:, :early]) + overlap(values_low_b, applied_b)
     ) / float(cell_count)
     select_full = (target[:, None] == jnp.arange(group_size, dtype=jnp.int32)[None, :]).astype(
         jnp.float32
@@ -104,25 +150,24 @@
         ],
         axis=1,
     ).reshape(domain_count, capacity, group_size + 1)
-    got_ham = lax.all_to_all(send_ham, "dom", split_axis=0, concat_axis=0, tiled=True).reshape(
+    shared_ham = lax.all_gather(send_ham, "dom", axis=0, tiled=True).reshape(
+        domain_count, domain_count, capacity, group_size + 1
+    )
+    got_ham = lax.dynamic_slice_in_dim(shared_ham, lax.axis_index("dom"), 1, axis=1).reshape(
         domain_count * capacity, group_size + 1
     )
     got_rows = got_ham[:, group_size]
-    piece_of_place = jnp.sum(
-        jnp.where(place_hot, jnp.arange(slot_count, dtype=jnp.int32)[None, :], 0), axis=1
-    )
-    send_grad = jnp.take(
-        gradient_piece.reshape(slot_count, NB, plane_cells), piece_of_place, axis=0, mode="clip"
-    ).reshape(domain_count, capacity * NB, plane_cells)
-    got_grad = lax.all_to_all(send_grad, "dom", split_axis=0, concat_axis=0, tiled=True).reshape(
-        domain_count * capacity, NB, plane_cells
-    )
     row_hot = got_rows[None, :] == jnp.arange(owned_count, dtype=jnp.float32)[:, None]
     hamilton = jnp.dot(
         row_hot.astype(jnp.float32), got_ham[:, :group_size], precision=lax.Precision.HIGHEST
     )
-    gradient = jnp.einsum(
-        "rs,syc->ryc", row_hot.astype(jnp.bfloat16), got_grad, preferred_element_type=jnp.float32
+    row_low = row_hot.astype(jnp.bfloat16)
+    gradient = jnp.concatenate(
+        [
+            jnp.einsum("rs,syc->ryc", row_low, got, preferred_element_type=jnp.float32)
+            for got in (got_grad_a, got_grad_b)
+        ],
+        axis=2,
     ).reshape(owned_count, cell_count)
     return (gradient, hamilton)
 

time: 274 us -> 329 us (1.20)
  waiting for transfers between devices: 129 us -> 177 us
    all_gather x1 -> x3, waiting for transfers between devices: 29.2 us -> 176 us  [the longest x1 89.8 us: on_device(): lax.all_gather(send_ham, 'dom', axis=0, tiled=True)]
    all_to_all x2, waiting for transfers between devices: 100 us -> 0.01 us  [send_gradient(): got = lax.all_to_all(send, 'dom', split_axis=0, concat_axis=0, tiled=True)]
    slice x0 -> x5, local copies, waits for them, and re-layouts: none -> 7.5 us  [the longest x1 2.77 us: on_device(): window[:, :, :half]]
    unnamed x10 -> x33, local copies, waits for them, and re-layouts: 8.02 us -> 4.21 us
    reshape x3 -> x1, local copies, waits for them, and re-layouts: 3.59 us -> 0.05 us  [on_device(): lax.dynamic_slice_in_dim(shared_ham, lax.axis_index('dom'), 1, axis=1)]
    dot_general x9 -> x18, matrix products: 16.5 us -> 18.7 us  [the longest x2 3 us: overlap(): lax.dot_general(values_low.reshape(slot_count, NB, -1), applied.reshape(s...]
    gather x74 -> x76, local copies, waits for them, and re-layouts: 52.3 us -> 54.4 us
  transfers between devices with their start and end apart: 4 -> 6, of which waited for: 3 -> 3; matrix products, arithmetic and copies ran while one was open for 32% -> 36% of each run, Pallas kernels for 0% -> 0%
where the time goes in v3:
time: 329 us; the launch traced here: 328 us
  waiting for transfers between devices  177 us (54%)
  local copies, waits for them, and re-layouts  91.8 us (28%)
  matrix products  19.9 us (6%)
  between operations  14.2 us (4%)
  other arithmetic  13.9 us (4%)
  starting transfers between devices  10.9 us (3%)
    all_gather x1, waiting for transfers between devices, on_device(): lax.all_gather(send_ham, 'dom', axis=0, tiled=True)  89.8 us
    all_gather x1, waiting for transfers between devices, on_device(): gathered_b = lax.all_gather(blocks[:, :, half:], 'dom', axis=0, tiled=True)  74.4 us
    gather x72, local copies, waits for them, and re-layouts  43.7 us
    convert_element_type x1, local copies, waits for them, and re-layouts, spline_tables(): plane_value.astype(jnp.bfloat16)  12.4 us
    all_gather x1, waiting for transfers between devices, on_device(): gathered_a = lax.all_gather(blocks[:, :, :half], 'dom', axis=0, tiled=True)  12.1 us
    convert_element_type x1, local copies, waits for them, and re-layouts, spline_tables(): plane_curve.astype(jnp.bfloat16)  11.4 us
    all_to_all x2, starting transfers between devices, send_gradient(): got = lax.all_to_all(send, 'dom', split_axis=0, concat_axis=0, tiled=True)  10.8 us
    convert_element_type x1, other arithmetic, spline_tables(): plane_curve.astype(jnp.bfloat16)  7.63 us
  transfers between devices with their start and end apart: 6, of which 3 were waited for; matrix products, arithmetic and copies ran while one was open for 36% of the time, Pallas kernels for 0%

profile of v3, /device:TPU:8, one launch (start us, length us, event | category | flops | bytes accessed | tf_op | source)
XLA Modules:
  0.0 327.7 jit_solution(4178246686614464853)
XLA Ops:
  12.9 1.3 convert_reduce_fusion
  14.1 7.6 %fusion.1 = (bf16[32,32,32,32]{3,2,1,0:T(8,128)(2,1)}, bf16[32,32,32,32]{3,2,1,0:T(8,128)(2,1)}) fusion(f32[32,32]{1,0:T(8,128)S(1)} %copy.66, f32[32,32]{1,0:T(8,128)S(1)} %copy.63), kind=kLoop, calls=%fused_computation.9 | loop fusion | flops 6291456 | bytes 4202496 | tf_op jit(solution)/shard_map/convert_element_type | solution.py:33
  21.8 12.4 %convert_element_type.116 = bf16[1024,1024]{1,0:T(8,128)(2,1)} reshape(bf16[32,32,32,32]{3,2,1,0:T(8,128)(2,1)} %get-tuple-element.24) | data formatting | bytes 4194304 | tf_op jit(solution)/shard_map/convert_element_type | solution.py:32
  34.2 11.4 %convert_element_type.123 = bf16[1024,1024]{1,0:T(8,128)(2,1)S(1)} reshape(bf16[32,32,32,32]{3,2,1,0:T(8,128)(2,1)} %get-tuple-element.23) | data formatting | bytes 4194304 | tf_op jit(solution)/shard_map/convert_element_type | solution.py:33
  45.7 43.7 %while.1 = (s32[]{:T(128)}, f32[64,1024]{1,0:T(8,128)S(1)}, s32[24,2]{0,1:T(2,128)S(1)}, f32[24,32,1024]{2,1,0:T(8,128)}, s32[]{:T(128)}) while((s32[]{:T(128)}, f32[64,1024]{1,0:T(8,128)S(1)}, s32[24,2]{0,1:T(2,128)S(1)}, f32[24,32,1024]{2,1,0:T(8,128)}, s32[]{:T(128)}) %tuple.26), condition=%wide.while_cond, body=%wide.while_body.sunk | while | flops 2 | bytes 263257 | solution.py:68
  46.4 1.2 bitcast_dynamic-update-slice_fusion.2
  48.2 1.2 bitcast_dynamic-update-slice_fusion.2
  50.0 1.2 bitcast_dynamic-update-slice_fusion.2
  51.8 1.2 bitcast_dynamic-update-slice_fusion.2
  53.7 1.2 bitcast_dynamic-update-slice_fusion.2
  55.5 1.2 bitcast_dynamic-update-slice_fusion.2
  57.3 1.2 bitcast_dynamic-update-slice_fusion.2
  59.1 1.2 bitcast_dynamic-update-slice_fusion.2
  60.9 1.2 bitcast_dynamic-update-slice_fusion.2
  62.7 1.2 bitcast_dynamic-update-slice_fusion.2
  64.5 1.2 bitcast_dynamic-update-slice_fusion.2
  66.4 1.2 bitcast_dynamic-update-slice_fusion.2
  68.2 1.2 bitcast_dynamic-update-slice_fusion.2
  70.0 1.2 bitcast_dynamic-update-slice_fusion.2
  71.8 1.3 bitcast_dynamic-update-slice_fusion.2
  73.6 1.2 bitcast_dynamic-update-slice_fusion.2
  75.4 1.2 bitcast_dynamic-update-slice_fusion.2
  77.3 1.2 bitcast_dynamic-update-slice_fusion.2
  79.1 1.2 bitcast_dynamic-update-slice_fusion.2
  80.9 1.2 bitcast_dynamic-update-slice_fusion.2
  82.7 1.2 bitcast_dynamic-update-slice_fusion.2
  84.5 1.2 bitcast_dynamic-update-slice_fusion.2
  86.3 1.2 bitcast_dynamic-update-slice_fusion.2
  88.1 1.2 bitcast_dynamic-update-slice_fusion.2
  89.4 2.8 slice.45
  92.1 12.1 %all-gather.4.cloned.1.call-done = bf16[128,32,512]{2,1,0:T(8,128)(2,1)} async-done(((bf16[4,32,512]{2,1,0:T(8,128)(2,1)}), bf16[128,32,512]{2,1,0:T(8,128)(2,1)}) %all-gather.4.cloned.1.call-update) | async-done | bytes 4194320 | tf_op jit(solution)/shard_map/all_gather | solution.py:60
  104.3 3.7 %gather_fusion = bf16[24,32,512]{2,1,0:T(8,128)(2,1)} fusion(bf16[128,32,512]{2,1,0:T(8,128)(2,1)} %all-gather.4.cloned.1.call-done, s32[1024]{0:T(1024)S(1)} %pad_clamp_fusion.1), kind=kCustom, calls=%fused_computation | custom fusion | bytes 1572960 | tf_op jit(solution)/shard_map/jit(_take)/gather | solution.py:62
  108.0 1.7 convolution_convert_fusion.4
  114.6 1.9 gather_fusion.2
  116.5 5.6 %all-to-all-start = ((bf16[32,64,384]{2,1,0:T(8,128)(2,1)}), bf16[32,64,384]{2,1,0:T(8,128)(2,1)}, u32[]{:S(2)}, u32[]{:S(2)}) async-start(bf16[32,64,384]{2,1,0:T(8,128)(2,1)} %bitcast.33), calls=%async_computation | async-start | bytes 3145728 | tf_op jit(solution)/shard_map/all_to_all | solution.py:106
  122.1 1.7 slice.50
  124.8 74.4 %all-gather.6.cloned.1.call-done = bf16[128,32,512]{2,1,0:T(8,128)(2,1)} async-done(((bf16[4,32,512]{2,1,0:T(8,128)(2,1)}), bf16[128,32,512]{2,1,0:T(8,128)(2,1)}) %all-gather.6.cloned.1.call-update) | async-done | bytes 4194320 | tf_op jit(solution)/shard_map/all_gather | solution.py:61
  199.1 2.8 gather_fusion.1
  204.6 1.4 fusion.25
  206.0 2.4 fusion.100
  208.4 1.6 fusion.5
  210.0 1.4 fusion.14
  211.9 2.4 gather_fusion.3
  214.2 5.2 %all-to-all-start.1 = ((bf16[32,64,640]{2,1,0:T(8,128)(2,1)}), bf16[32,64,640]{2,1,0:T(8,128)(2,1)S(1)}, u32[]{:S(2)}, u32[]{:S(2)}) async-start(bf16[32,64,640]{2,1,0:T(8,128)(2,1)} %bitcast.116), calls=%async_computation.1 | async-start | bytes 5242880 | tf_op jit(solution)/shard_map/all_to_all | solution.py:106
  220.0 1.3 slice.104
  221.3 2.5 convolution_bitcast_fusion
  225.5 89.8 %all-gather.8.cloned.1.call-done = f32[1024,2,129]{2,0,1:T(8,128)} async-done(((f32[32,2,129]{2,0,1:T(8,128)}), f32[1024,2,129]{2,0,1:T(8,128)}) %all-gather.8.cloned.1.call-update) | async-done | bytes 1056784 | tf_op jit(solution)/shard_map/all_gather | solution.py:153
  317.3 2.0 fusion.12
  (133 shorter events, 34.7 us)
Async XLA Ops:
  7.2 97.1 %all-gather.4.cloned.1.call-start = ((), (), s32[]{:S(2)}) async-start(), calls=%async_computation.2 | async-start | bytes 4325376 | tf_op jit(solution)/shard_map/all_gather | solution.py:60
  9.0 190.2 %all-gather.6.cloned.1.call-start = ((), (), s32[]{:S(2)}) async-start(), calls=%async_computation.3 | async-start | bytes 4325376 | tf_op jit(solution)/shard_map/all_gather | solution.py:61
  9.0 36.6 %collective-permute-start = (f32[1,32,1024]{2,1,0:T(8,128)}, f32[1,32,1024]{2,1,0:T(8,128)S(1)}, u32[]{:S(2)}, u32[]{:S(2)}) collective-permute-start(f32[1,32,1024]{2,1,0:T(8,128)} %param.6), channel_id=1, source_target_pairs={{32,0},{64,32},{96,64},{128,96},{160,128},{192,160},{224,192},{256... | collective-permute-start | bytes 393224 | tf_op jit(solution)/shard_map/ppermute | solution.py:13
  34.2 11.4 %copy-start.13 = (f32[1,32,1024]{2,1,0:T(8,128)S(1)}, f32[1,32,1024]{2,1,0:T(8,128)}, u32[]{:S(2)}) copy-start(f32[1,32,1024]{2,1,0:T(8,128)} %param.6) | copy-start | bytes 393220
  45.6 66.0 %copy-start.1 = (bf16[1024,1024]{1,0:T(8,128)(2,1)}, bf16[1024,1024]{1,0:T(8,128)(2,1)S(1)}, u32[]{:S(2)}) copy-start(bf16[1024,1024]{1,0:T(8,128)(2,1)S(1)} %convert_element_type.123) | copy-start | bytes 6291460
  108.0 1.7 copy-start.3
  108.0 2.2 copy-start.7
  110.1 0.9 copy-start.4
  110.7 2.6 copy-start
  110.7 2.0 copy-start.6
  113.4 0.9 copy-start.9
  116.5 97.7 %all-to-all-start = ((bf16[32,64,384]{2,1,0:T(8,128)(2,1)}), bf16[32,64,384]{2,1,0:T(8,128)(2,1)}, u32[]{:S(2)}, u32[]{:S(2)}) async-start(bf16[32,64,384]{2,1,0:T(8,128)(2,1)} %bitcast.33), calls=%async_computation | async-start | bytes 3145728 | tf_op jit(solution)/shard_map/all_to_all | solution.py:106
  122.1 1.8 copy-start.10
  202.3 1.1 copy-start.5
  203.0 1.7 copy-start.8
  206.0 2.4 copy-start.2
  208.4 1.6 copy-start.12
  210.0 1.4 copy-start.11
  214.2 5.3 %copy-start.14 = (s32[64]{0:T(128)S(1)}, s32[64]{0:T(128)}, u32[]{:S(2)}) copy-start(s32[64]{0:T(128)} %get-tuple-element.10) | copy-start | bytes 772
  214.2 5.3 %copy-start.15 = (s32[64]{0:T(128)S(1)}, s32[64]{0:T(128)}, u32[]{:S(2)}) copy-start(s32[64]{0:T(128)} %get-tuple-element.12) | copy-start | bytes 772
  214.2 105.1 %all-to-all-start.1 = ((bf16[32,64,640]{2,1,0:T(8,128)(2,1)}), bf16[32,64,640]{2,1,0:T(8,128)(2,1)S(1)}, u32[]{:S(2)}, u32[]{:S(2)}) async-start(bf16[32,64,640]{2,1,0:T(8,128)(2,1)} %bitcast.116), calls=%async_computation.1 | async-start | bytes 5242880 | tf_op jit(solution)/shard_map/all_to_all | solution.py:106
  219.5 95.8 %all-gather.8.cloned.1.call-start = ((), (), s32[]{:S(2)}) async-start(), calls=%async_computation.4 | async-start | bytes 2162688 | tf_op jit(solution)/shard_map/all_gather | solution.py:153
Sparse Core Ops, SparseCore 0:
  11.7 92.5 all-gather.3
  107.5 91.6 all-gather.5
  225.6 89.6 all-gather.7

commit v4 on v3

--- a/solution.py
+++ b/solution.py
@@ -57,9 +57,19 @@
     blocks = owned_blips.reshape(owned_count, NB, plane_cells)
     half = plane_cells // 2
     early = half - 4 * NB
-    gathered_a = lax.all_gather(blocks[:, :, :half], "dom", axis=0, tiled=True)
+    asked_of_me = lax.all_to_all(
+        asked_rows.reshape(domain_count, capacity), "dom", split_axis=0, concat_axis=0, tiled=True
+    ).reshape(-1)
+    lent = jnp.take(blocks[:, :, :half], asked_of_me, axis=0, mode="clip")
+    fetched_a = lax.all_to_all(
+        lent.reshape(domain_count, capacity * NB, half),
+        "dom",
+        split_axis=0,
+        concat_axis=0,
+        tiled=True,
+    ).reshape(domain_count * capacity, NB, half)
     gathered_b = lax.all_gather(blocks[:, :, half:], "dom", axis=0, tiled=True)
-    blips_a = jnp.take(gathered_a, target, axis=0, mode="clip")
+    blips_a = jnp.take(fetched_a, place_slot, axis=0, mode="clip")
     blips_b = jnp.take(gathered_b, target, axis=0, mode="clip")
     upper_cells = passed_along(potential, "grp", -1)
     extended = jnp.concatenate([potential[0], upper_cells[0]], axis=0)
@@ -142,25 +152,14 @@
         jnp.float32
     )
     weighted = jnp.dot(intersection, select_full, precision=lax.Precision.HIGHEST)
-    place_f32 = place_hot.astype(jnp.float32)
-    send_ham = jnp.concatenate(
-        [
-            jnp.dot(place_f32, weighted, precision=lax.Precision.HIGHEST),
-            asked_rows.astype(jnp.float32)[:, None],
-        ],
-        axis=1,
-    ).reshape(domain_count, capacity, group_size + 1)
-    shared_ham = lax.all_gather(send_ham, "dom", axis=0, tiled=True).reshape(
-        domain_count, domain_count, capacity, group_size + 1
+    send_ham = jnp.dot(
+        place_hot.astype(jnp.float32), weighted, precision=lax.Precision.HIGHEST
+    ).reshape(domain_count, capacity, group_size)
+    got_ham = lax.all_to_all(send_ham, "dom", split_axis=0, concat_axis=0, tiled=True).reshape(
+        domain_count * capacity, group_size
     )
-    got_ham = lax.dynamic_slice_in_dim(shared_ham, lax.axis_index("dom"), 1, axis=1).reshape(
-        domain_count * capacity, group_size + 1
-    )
-    got_rows = got_ham[:, group_size]
-    row_hot = got_rows[None, :] == jnp.arange(owned_count, dtype=jnp.float32)[:, None]
-    hamilton = jnp.dot(
-        row_hot.astype(jnp.float32), got_ham[:, :group_size], precision=lax.Precision.HIGHEST
-    )
+    row_hot = asked_of_me[None, :] == jnp.arange(owned_count, dtype=jnp.int32)[:, None]
+    hamilton = jnp.dot(row_hot.astype(jnp.float32), got_ham, precision=lax.Precision.HIGHEST)
     row_low = row_hot.astype(jnp.bfloat16)
     gradient = jnp.concatenate(
         [

time: 329 us -> 292 us (0.89)
  the two profiles are of different devices: /device:TPU:8 before, /device:TPU:40 now
where the time goes in v4:
time: 292 us; the launch traced here: 290 us
  waiting for transfers between devices  104 us (36%)
  local copies, waits for them, and re-layouts  94.2 us (32%)
  starting transfers between devices  43 us (15%)
  matrix products  21 us (7%)
  between operations  14.4 us (5%)
  other arithmetic  13.3 us (5%)
    all_to_all x2, waiting for transfers between devices, send_gradient(): got = lax.all_to_all(send, 'dom', split_axis=0, concat_axis=0, tiled=True)  83.8 us
    gather x72, local copies, waits for them, and re-layouts  46.6 us
    all_to_all x2, starting transfers between devices, send_gradient(): got = lax.all_to_all(send, 'dom', split_axis=0, concat_axis=0, tiled=True)  13.9 us
    all_to_all x1, starting transfers between devices, on_device(): lax.all_to_all(asked_rows.reshape(domain_count, capacity), 'dom', split_a...  13.2 us
    all_to_all x1, waiting for transfers between devices, on_device(): lax.all_to_all(lent.reshape(domain_count, capacity * NB, half), 'dom', sp...  13 us
    convert_element_type x1, local copies, waits for them, and re-layouts, spline_tables(): plane_value.astype(jnp.bfloat16)  12.4 us
    convert_element_type x1, local copies, waits for them, and re-layouts, spline_tables(): plane_curve.astype(jnp.bfloat16)  12.4 us
    all_to_all x1, starting transfers between devices, on_device(): lax.all_to_all(lent.reshape(domain_count, capacity * NB, half), 'dom', sp...  9.78 us
  transfers between devices with their start and end apart: 7, of which 4 were waited for; matrix products, arithmetic and copies ran while one was open for 41% of the time, Pallas kernels for 0%

profile of v4, /device:TPU:40, one launch (start us, length us, event | category | flops | bytes accessed | tf_op | source)
XLA Modules:
  0.0 290.0 jit_solution(8179691871241928049)
XLA Ops:
  10.9 13.2 %all-to-all-start = ((s32[32,1,2]{2,1,0:T(1,128)}), s32[32,1,2]{2,1,0:T(1,128)S(1)}, u32[]{:S(2)}, u32[]{:S(2)}) async-start(s32[32,1,2]{2,1,0:T(1,128)} %bitcast.1), calls=%async_computation | async-start | bytes 32768 | tf_op jit(solution)/shard_map/all_to_all | solution.py:60
  27.2 7.6 %fusion.1 = (bf16[32,32,32,32]{3,2,1,0:T(8,128)(2,1)}, bf16[32,32,32,32]{3,2,1,0:T(8,128)(2,1)}) fusion(f32[32,32]{1,0:T(8,128)S(1)} %copy.45, f32[32,32]{1,0:T(8,128)S(1)} %copy.42), kind=kLoop, calls=%fused_computation.10 | loop fusion | flops 6291456 | bytes 4202496 | tf_op jit(solution)/shard_map/convert_element_type | solution.py:33
  34.9 12.4 %convert_element_type.103 = bf16[1024,1024]{1,0:T(8,128)(2,1)} reshape(bf16[32,32,32,32]{3,2,1,0:T(8,128)(2,1)} %get-tuple-element.24) | data formatting | bytes 4194304 | tf_op jit(solution)/shard_map/convert_element_type | solution.py:32
  47.3 12.4 %convert_element_type.109 = bf16[1024,1024]{1,0:T(8,128)(2,1)} reshape(bf16[32,32,32,32]{3,2,1,0:T(8,128)(2,1)} %get-tuple-element.23) | data formatting | bytes 4194304 | tf_op jit(solution)/shard_map/convert_element_type | solution.py:33
  61.1 2.0 gather_fusion
  63.1 9.8 %all-to-all-start.1 = ((bf16[32,64,512]{2,1,0:T(8,128)(2,1)}), bf16[32,64,512]{2,1,0:T(8,128)(2,1)}, u32[]{:S(2)}, u32[]{:S(2)}) async-start(bf16[32,64,512]{2,1,0:T(8,128)(2,1)} %bitcast.3), calls=%async_computation.1 | async-start | bytes 4194304 | tf_op jit(solution)/shard_map/all_to_all | solution.py:64
  72.9 46.6 %while.1 = (s32[]{:T(128)}, f32[64,1024]{1,0:T(8,128)S(1)}, s32[24,2]{0,1:T(2,128)S(1)}, f32[24,32,1024]{2,1,0:T(8,128)}, s32[]{:T(128)}) while((s32[]{:T(128)}, f32[64,1024]{1,0:T(8,128)S(1)}, s32[24,2]{0,1:T(2,128)S(1)}, f32[24,32,1024]{2,1,0:T(8,128)}, s32[]{:T(128)}) %tuple.26), condition=%wide.while_cond, body=%wide.while_body.sunk | while | flops 2 | bytes 263257 | solution.py:78
  73.6 1.3 bitcast_dynamic-update-slice_fusion.2
  75.5 1.3 bitcast_dynamic-update-slice_fusion.2
  77.4 1.3 bitcast_dynamic-update-slice_fusion.2
  81.3 1.3 bitcast_dynamic-update-slice_fusion.2
  83.3 1.3 bitcast_dynamic-update-slice_fusion.2
  85.2 1.3 bitcast_dynamic-update-slice_fusion.2
  87.2 1.3 bitcast_dynamic-update-slice_fusion.2
  89.1 1.3 bitcast_dynamic-update-slice_fusion.2
  91.1 1.3 bitcast_dynamic-update-slice_fusion.2
  93.0 1.3 bitcast_dynamic-update-slice_fusion.2
  95.0 1.3 bitcast_dynamic-update-slice_fusion.2
  98.8 1.3 bitcast_dynamic-update-slice_fusion.2
  102.7 1.3 bitcast_dynamic-update-slice_fusion.2
  106.6 1.3 bitcast_dynamic-update-slice_fusion.2
  108.5 1.3 bitcast_dynamic-update-slice_fusion.2
  110.5 1.3 bitcast_dynamic-update-slice_fusion.2
  114.3 1.3 bitcast_dynamic-update-slice_fusion.2
  116.3 1.3 bitcast_dynamic-update-slice_fusion.2
  118.2 1.3 bitcast_dynamic-update-slice_fusion.2
  119.5 1.8 slice.44
  122.0 1.3 slice.38
  123.4 13.0 %all-to-all-done.1 = bf16[32,64,512]{2,1,0:T(8,128)(2,1)} async-done(((bf16[32,64,512]{2,1,0:T(8,128)(2,1)}), bf16[32,64,512]{2,1,0:T(8,128)(2,1)}, u32[]{:S(2)}, u32[]{:S(2)}) %all-to-all-start.1) | async-done | bytes 2097184 | tf_op jit(solution)/shard_map/all_to_all | solution.py:64
  136.3 2.2 gather_fusion.1
  139.0 1.6 fusion.34
  142.8 1.6 fusion.36
  144.4 1.8 fusion.11
  147.1 1.6 convolution_convert_fusion.6
  149.0 1.9 gather_fusion.2
  150.9 9.8 %all-to-all-start.2 = ((bf16[32,64,384]{2,1,0:T(8,128)(2,1)}), bf16[32,64,384]{2,1,0:T(8,128)(2,1)}, u32[]{:S(2)}, u32[]{:S(2)}) async-start(bf16[32,64,384]{2,1,0:T(8,128)(2,1)} %bitcast.130), calls=%async_computation.2 | async-start | bytes 3145728 | tf_op jit(solution)/shard_map/all_to_all | solution.py:116
  160.8 2.8 gather_fusion.3
  166.3 1.4 fusion.27
  167.7 1.4 fusion.100
  169.3 1.6 fusion.5
  173.7 1.4 fusion.14
  175.1 24.7 %all-to-all-done.2 = bf16[32,64,384]{2,1,0:T(8,128)(2,1)} async-done(((bf16[32,64,384]{2,1,0:T(8,128)(2,1)}), bf16[32,64,384]{2,1,0:T(8,128)(2,1)}, u32[]{:S(2)}, u32[]{:S(2)}) %all-to-all-start.2) | async-done | bytes 1572896 | tf_op jit(solution)/shard_map/all_to_all | solution.py:116
  199.9 5.6 %all-to-all-start.4 = ((f32[32,2,128]{2,1,0:T(2,128)}), f32[32,2,128]{2,1,0:T(2,128)S(1)}, u32[]{:S(2)}, u32[]{:S(2)}) async-start(f32[32,2,128]{2,1,0:T(2,128)} %bitcast.43), calls=%async_computation.4 | async-start | bytes 65536 | tf_op jit(solution)/shard_map/all_to_all | solution.py:158
  205.9 2.4 gather_fusion.4
  208.3 7.2 %all-to-all-done.4 = f32[32,2,128]{2,1,0:T(2,128)S(1)} async-done(((f32[32,2,128]{2,1,0:T(2,128)}), f32[32,2,128]{2,1,0:T(2,128)S(1)}, u32[]{:S(2)}, u32[]{:S(2)}) %all-to-all-start.4) | async-done | bytes 32800 | tf_op jit(solution)/shard_map/all_to_all | solution.py:158
  215.4 4.1 %all-to-all-start.3 = ((bf16[32,64,640]{2,1,0:T(8,128)(2,1)}), bf16[32,64,640]{2,1,0:T(8,128)(2,1)S(1)}, u32[]{:S(2)}, u32[]{:S(2)}) async-start(bf16[32,64,640]{2,1,0:T(8,128)(2,1)} %bitcast.124), calls=%async_computation.3 | async-start | bytes 5242880 | tf_op jit(solution)/shard_map/all_to_all | solution.py:116
  219.5 2.0 fusion.12
  222.2 59.1 %all-to-all-done.3 = bf16[32,64,640]{2,1,0:T(8,128)(2,1)S(1)} async-done(((bf16[32,64,640]{2,1,0:T(8,128)(2,1)}), bf16[32,64,640]{2,1,0:T(8,128)(2,1)S(1)}, u32[]{:S(2)}, u32[]{:S(2)}) %all-to-all-start.3) | async-done | bytes 2621472 | tf_op jit(solution)/shard_map/all_to_all | solution.py:116
  (125 shorter events, 43.3 us)
Async XLA Ops:
  9.5 25.4 %copy-start.9 = (s32[24]{0:T(128)}, s32[24]{0:T(128)S(1)}, u32[]{:S(2)}) copy-start(s32[24]{0:T(128)S(1)} %get-tuple-element.26) | copy-start | bytes 292
  10.9 48.8 %all-to-all-start = ((s32[32,1,2]{2,1,0:T(1,128)}), s32[32,1,2]{2,1,0:T(1,128)S(1)}, u32[]{:S(2)}, u32[]{:S(2)}) async-start(s32[32,1,2]{2,1,0:T(1,128)} %bitcast.1), calls=%async_computation | async-start | bytes 32768 | tf_op jit(solution)/shard_map/all_to_all | solution.py:60
  24.1 136.7 %all-gather.2.cloned.1.call-start = ((), (), s32[]{:S(2)}) async-start(), calls=%async_computation.5 | async-start | bytes 4325376 | tf_op jit(solution)/shard_map/all_gather | solution.py:71
  25.9 47.0 %collective-permute-start = (f32[1,32,1024]{2,1,0:T(8,128)}, f32[1,32,1024]{2,1,0:T(8,128)S(1)}, u32[]{:S(2)}, u32[]{:S(2)}) collective-permute-start(f32[1,32,1024]{2,1,0:T(8,128)} %param.6), channel_id=1, source_target_pairs={{32,0},{64,32},{96,64},{128,96},{160,128},{192,160},{224,192},{256... | collective-permute-start | bytes 393224 | tf_op jit(solution)/shard_map/ppermute | solution.py:13
  27.2 7.6 %copy-start.11 = (s32[24]{0:T(128)S(1)}, s32[24]{0:T(128)}, u32[]{:S(2)}) copy-start(s32[24]{0:T(128)} %param.9) | copy-start | bytes 292
  63.1 9.8 %copy-start.8 = (f32[1,32,1024]{2,1,0:T(8,128)S(1)}, f32[1,32,1024]{2,1,0:T(8,128)}, u32[]{:S(2)}) copy-start(f32[1,32,1024]{2,1,0:T(8,128)} %param.6) | copy-start | bytes 393220
  63.1 73.3 %all-to-all-start.1 = ((bf16[32,64,512]{2,1,0:T(8,128)(2,1)}), bf16[32,64,512]{2,1,0:T(8,128)(2,1)}, u32[]{:S(2)}, u32[]{:S(2)}) async-start(bf16[32,64,512]{2,1,0:T(8,128)(2,1)} %bitcast.3), calls=%async_computation.1 | async-start | bytes 4194304 | tf_op jit(solution)/shard_map/all_to_all | solution.py:64
  119.5 2.5 copy-start.5
  141.5 2.9 %copy-start.3 = (f32[24,32,512]{2,1,0:T(8,128)S(1)}, f32[24,32,512]{2,1,0:T(8,128)}, u32[]{:S(2)}) copy-start(f32[24,32,512]{2,1,0:T(8,128)} %slice.38) | copy-start | bytes 4718596
  141.9 0.9 copy-start.1
  150.9 49.0 %all-to-all-start.2 = ((bf16[32,64,384]{2,1,0:T(8,128)(2,1)}), bf16[32,64,384]{2,1,0:T(8,128)(2,1)}, u32[]{:S(2)}, u32[]{:S(2)}) async-start(bf16[32,64,384]{2,1,0:T(8,128)(2,1)} %bitcast.130), calls=%async_computation.2 | async-start | bytes 3145728 | tf_op jit(solution)/shard_map/all_to_all | solution.py:116
  164.0 1.1 copy-start.2
  164.6 1.7 copy-start.4
  167.7 1.6 copy-start
  170.8 1.1 copy-start.6
  170.9 1.2 copy-start.7
  170.9 1.8 copy-start.10
  199.9 15.5 %all-to-all-start.4 = ((f32[32,2,128]{2,1,0:T(2,128)}), f32[32,2,128]{2,1,0:T(2,128)S(1)}, u32[]{:S(2)}, u32[]{:S(2)}) async-start(f32[32,2,128]{2,1,0:T(2,128)} %bitcast.43), calls=%async_computation.4 | async-start | bytes 65536 | tf_op jit(solution)/shard_map/all_to_all | solution.py:158
  215.4 65.8 %all-to-all-start.3 = ((bf16[32,64,640]{2,1,0:T(8,128)(2,1)}), bf16[32,64,640]{2,1,0:T(8,128)(2,1)S(1)}, u32[]{:S(2)}, u32[]{:S(2)}) async-start(bf16[32,64,640]{2,1,0:T(8,128)(2,1)} %bitcast.124), calls=%async_computation.3 | async-start | bytes 5242880 | tf_op jit(solution)/shard_map/all_to_all | solution.py:116
Sparse Core Ops, SparseCore 0:
  28.6 113.8 all-gather.1

commit v5 on v4

--- a/solution.py
+++ b/solution.py
@@ -13,19 +13,21 @@
     return lax.ppermute(block, axis, route)
 
 
+def line_tables(offset):
+    spline = jnp.where(offset == 0, 2.0 / 3.0, jnp.where(jnp.abs(offset) == 1, 1.0 / 6.0, 0.0))
+    second = jnp.where(offset == 0, -2.0, jnp.where(jnp.abs(offset) == 1, 1.0, 0.0))
+    return spline.astype(jnp.float32), second.astype(jnp.float32)
+
+
 def spline_tables():
     cells_line = jnp.arange(NB, dtype=jnp.int32)
-    offset = cells_line[:, None] - cells_line[None, :]
-    spline = jnp.where(
-        offset == 0, 2.0 / 3.0, jnp.where(jnp.abs(offset) == 1, 1.0 / 6.0, 0.0)
-    ).astype(jnp.float32)
-    second = jnp.where(offset == 0, -2.0, jnp.where(jnp.abs(offset) == 1, 1.0, 0.0)).astype(
-        jnp.float32
-    )
-    plane_value = jnp.einsum("ac,bd->abcd", spline, spline).reshape(NB * NB, NB * NB)
-    plane_curve = (
-        jnp.einsum("ac,bd->abcd", second, spline) + jnp.einsum("ac,bd->abcd", spline, second)
-    ).reshape(NB * NB, NB * NB)
+    spline, second = line_tables(cells_line[:, None] - cells_line[None, :])
+    rows = lax.broadcasted_iota(jnp.int32, (NB * NB, NB * NB), 0)
+    cols = lax.broadcasted_iota(jnp.int32, (NB * NB, NB * NB), 1)
+    spline_x, second_x = line_tables(rows // NB - cols // NB)
+    spline_z, second_z = line_tables(rows % NB - cols % NB)
+    plane_value = spline_x * spline_z
+    plane_curve = second_x * spline_z + spline_x * second_z
     return (
         spline.astype(jnp.bfloat16),
         second.astype(jnp.bfloat16),
@@ -55,8 +57,8 @@
         1 - jnp.sum(place_hot.astype(jnp.int32), axis=1)
     )
     blocks = owned_blips.reshape(owned_count, NB, plane_cells)
-    half = plane_cells // 2
-    early = half - 4 * NB
+    half = 3 * plane_cells // 8
+    early = plane_cells // 4
     asked_of_me = lax.all_to_all(
         asked_rows.reshape(domain_count, capacity), "dom", split_axis=0, concat_axis=0, tiled=True
     ).reshape(-1)
@@ -74,10 +76,9 @@
     upper_cells = passed_along(potential, "grp", -1)
     extended = jnp.concatenate([potential[0], upper_cells[0]], axis=0)
 
-    def cut_window(first_row):
-        return lax.dynamic_slice_in_dim(extended, first_row, NB, 0)
-
-    window = jax.vmap(cut_window)(slot_offset)
+    window = jnp.take(
+        extended, slot_offset[:, None] + jnp.arange(NB, dtype=jnp.int32)[None, :], axis=0, mode="clip"
+    )
 
     def y_pass(table, layered):
         return jnp.einsum(

time: 292 us -> 250 us (0.86)
  the two profiles are of different devices: /device:TPU:40 before, /device:TPU:8 now
where the time goes in v5:
time: 250 us; the launch traced here: 249 us
  waiting for transfers between devices  142 us (57%)
  starting transfers between devices  36 us (14%)
  local copies, waits for them, and re-layouts  23.7 us (9%)
  matrix products  22.9 us (9%)
  between operations  14.5 us (6%)
  other arithmetic  10.4 us (4%)
    all_to_all x2, waiting for transfers between devices, send_gradient(): got = lax.all_to_all(send, 'dom', split_axis=0, concat_axis=0, tiled=True)  65 us
    all_to_all x1, waiting for transfers between devices, on_device(): lax.all_to_all(lent.reshape(domain_count, capacity * NB, half), 'dom', sp...  31.8 us
    all_gather x1, waiting for transfers between devices, on_device(): gathered_b = lax.all_gather(blocks[:, :, half:], 'dom', axis=0, tiled=True)  27.9 us
    all_to_all x1, starting transfers between devices, on_device(): lax.all_to_all(asked_rows.reshape(domain_count, capacity), 'dom', split_a...  13.2 us
    all_to_all x2, starting transfers between devices, send_gradient(): got = lax.all_to_all(send, 'dom', split_axis=0, concat_axis=0, tiled=True)  10.8 us
    all_to_all x1, waiting for transfers between devices, on_device(): lax.all_to_all(asked_rows.reshape(domain_count, capacity), 'dom', split_a...  9.73 us
    all_to_all x1, starting transfers between devices, on_device(): lax.all_to_all(send_ham, 'dom', split_axis=0, concat_axis=0, tiled=True)  7.12 us
    all_to_all x1, waiting for transfers between devices, on_device(): lax.all_to_all(send_ham, 'dom', split_axis=0, concat_axis=0, tiled=True)  7.05 us
  transfers between devices with their start and end apart: 7, of which 5 were waited for; matrix products, arithmetic and copies ran while one was open for 20% of the time, Pallas kernels for 0%

profile of v5, /device:TPU:8, one launch (start us, length us, event | category | flops | bytes accessed | tf_op | source)
XLA Modules:
  0.0 249.0 jit_solution(8866552671979374495)
XLA Ops:
  7.2 1.0 copy.73
  8.2 0.7 slice.70
  8.9 0.7 fusion.56
  9.7 0.8 select_reduce_fusion.2
  10.5 0.7 multiply_add_fusion.2
  11.2 0.7 select_reduce_fusion
  12.0 0.7 add.108
  12.7 13.2 %all-to-all-start = ((s32[32,1,2]{2,1,0:T(1,128)}), s32[32,1,2]{2,1,0:T(1,128)S(1)}, u32[]{:S(2)}, u32[]{:S(2)}) async-start(s32[32,1,2]{2,1,0:T(1,128)} %bitcast.1), calls=%async_computation | async-start | bytes 32768 | tf_op jit(solution)/shard_map/all_to_all | solution.py:62
  25.9 9.7 %all-to-all-done = s32[32,1,2]{2,1,0:T(1,128)S(1)} async-done(((s32[32,1,2]{2,1,0:T(1,128)}), s32[32,1,2]{2,1,0:T(1,128)S(1)}, u32[]{:S(2)}, u32[]{:S(2)}) %all-to-all-start) | async-done | bytes 288 | tf_op jit(solution)/shard_map/all_to_all | solution.py:62
  35.6 0.5 broadcast.247
  36.1 0.7 reduce.3
  36.9 1.9 gather_fusion
  38.9 4.8 %all-to-all-start.1 = ((bf16[32,64,384]{2,1,0:T(8,128)(2,1)}), bf16[32,64,384]{2,1,0:T(8,128)(2,1)}, u32[]{:S(2)}, u32[]{:S(2)}) async-start(bf16[32,64,384]{2,1,0:T(8,128)(2,1)} %bitcast.3), calls=%async_computation.1 | async-start | bytes 3145728 | tf_op jit(solution)/shard_map/all_to_all | solution.py:66
  44.0 5.2 %add_convert_fusion = (bf16[1024,1024]{1,0:T(8,128)(2,1)}, bf16[1024,1024]{1,0:T(8,128)(2,1)}) fusion(s32[1024]{0:T(1024)S(1)} %get-tuple-element.14, s32[1024]{0:T(1024)S(1)} %get-tuple-element.15, s32[1024]{0:T(1024)S(1)} %get-tuple-element.13, s32[1024]{0:T(1024)S(1)} %get-tuple-element.16, pred[1024]{0:T(1024)(128)(4,1)S(1)} %get-tuple-element.17, ...), kind=kLoop, calls=%fused_computation.6 | loop fusion | flops 27262976 | bytes 4212736 | tf_op jit(solution)/shard_map/convert_element_type | solution.py:35
  49.2 2.6 %gather_fusion.2 = f32[768,1024]{1,0:T(8,128)S(1)} fusion(f32[64,1024]{1,0:T(8,128)S(1)} %pad_maximum_fusion.3, s32[1024]{0:T(1024)S(1)} %pad_clamp_fusion.2), kind=kCustom, calls=%fused_computation.2 | custom fusion | bytes 6294528 | tf_op jit(solution)/shard_map/jit(_take)/gather | solution.py:79
  51.8 1.2 slice.67
  53.0 1.7 slice.73
  54.6 31.8 %all-to-all-done.1 = bf16[32,64,384]{2,1,0:T(8,128)(2,1)} async-done(((bf16[32,64,384]{2,1,0:T(8,128)(2,1)}), bf16[32,64,384]{2,1,0:T(8,128)(2,1)}, u32[]{:S(2)}, u32[]{:S(2)}) %all-to-all-start.1) | async-done | bytes 1572896 | tf_op jit(solution)/shard_map/all_to_all | solution.py:66
  86.5 2.1 gather_fusion.1
  89.3 0.5 copy-done.3
  89.8 0.5 fusion.51
  90.4 0.5 bitcast_multiply_fusion.1
  90.9 1.5 fusion.20
  92.4 0.8 slice.92
  93.9 1.6 gather_fusion.3
  95.5 6.5 %all-to-all-start.2 = ((bf16[32,64,256]{2,1,0:T(8,128)(2,1)}), bf16[32,64,256]{2,1,0:T(8,128)(2,1)}, u32[]{:S(2)}, u32[]{:S(2)}) async-start(bf16[32,64,256]{2,1,0:T(8,128)(2,1)} %bitcast.109), calls=%async_computation.2 | async-start | bytes 2097152 | tf_op jit(solution)/shard_map/all_to_all | solution.py:117
  102.0 0.6 convolution_bitcast_fusion
  102.6 27.9 %all-gather.2.cloned.1.call-done = bf16[128,32,640]{2,1,0:T(8,128)(2,1)} async-done(((bf16[4,32,640]{2,1,0:T(8,128)(2,1)}), bf16[128,32,640]{2,1,0:T(8,128)(2,1)}) %all-gather.2.cloned.1.call-update) | async-done | bytes 5242896 | tf_op jit(solution)/shard_map/all_gather | solution.py:73
  130.5 4.2 %gather_fusion.4 = bf16[24,32,640]{2,1,0:T(8,128)(2,1)} fusion(bf16[128,32,640]{2,1,0:T(8,128)(2,1)} %all-gather.2.cloned.1.call-done, s32[1024]{0:T(1024)S(1)} %pad_clamp_fusion), kind=kCustom, calls=%fused_computation.4 | custom fusion | bytes 1966176 | tf_op jit(solution)/shard_map/jit(_take)/gather | solution.py:75
  134.6 1.8 fusion.18
  136.4 0.5 fusion.19
  137.1 1.4 fusion.131
  138.8 1.3 copy-done.6
  140.1 1.4 fusion.6
  141.8 1.5 fusion.5
  143.3 3.0 %fusion.39 = f32[24,24]{1,0:T(8,128)S(1)} fusion(f32[24,24]{1,0:T(8,128)S(1)} %convolution_bitcast_fusion, bf16[24,32,768]{2,1,0:T(8,128)(2,1)S(1)} %bitcast.114, bf16[24,32,768]{2,1,0:T(8,128)(2,1)S(1)} %bitcast.126), kind=kOutput, calls=%fused_computation.56 | convolution fusion | flops 28312704 | bytes 2363904 | tf_op jit(solution)/shard_map/dot_general | solution.py:142
  146.6 0.9 fusion.55
  147.5 1.4 fusion.12
  148.9 7.1 %all-to-all-start.4 = ((f32[32,2,128]{2,1,0:T(2,128)}), f32[32,2,128]{2,1,0:T(2,128)S(1)}, u32[]{:S(2)}, u32[]{:S(2)}) async-start(f32[32,2,128]{2,1,0:T(2,128)} %bitcast.41), calls=%async_computation.4 | async-start | bytes 65536 | tf_op jit(solution)/shard_map/all_to_all | solution.py:159
  156.0 0.4 fusion.16
  156.5 2.4 gather_fusion.5
  158.9 7.1 %all-to-all-done.4 = f32[32,2,128]{2,1,0:T(2,128)S(1)} async-done(((f32[32,2,128]{2,1,0:T(2,128)}), f32[32,2,128]{2,1,0:T(2,128)S(1)}, u32[]{:S(2)}, u32[]{:S(2)}) %all-to-all-start.4) | async-done | bytes 32800 | tf_op jit(solution)/shard_map/all_to_all | solution.py:159
  165.9 4.3 %all-to-all-start.3 = ((bf16[32,64,768]{2,1,0:T(8,128)(2,1)}), bf16[32,64,768]{2,1,0:T(8,128)(2,1)S(1)}, u32[]{:S(2)}, u32[]{:S(2)}) async-start(bf16[32,64,768]{2,1,0:T(8,128)(2,1)} %bitcast.101), calls=%async_computation.3 | async-start | bytes 6291456 | tf_op jit(solution)/shard_map/all_to_all | solution.py:117
  170.2 1.9 fusion.44
  172.1 0.7 fusion.92
  172.8 65.0 %all-to-all-done.3 = bf16[32,64,768]{2,1,0:T(8,128)(2,1)S(1)} async-done(((bf16[32,64,768]{2,1,0:T(8,128)(2,1)}), bf16[32,64,768]{2,1,0:T(8,128)(2,1)S(1)}, u32[]{:S(2)}, u32[]{:S(2)}) %all-to-all-start.3) | async-done | bytes 3145760 | tf_op jit(solution)/shard_map/all_to_all | solution.py:117
  237.8 3.4 %fusion.2 = f32[4,32,768]{2,0,1:T(4,128)S(1)} fusion(bf16[64,32,768]{2,1,0:T(8,128)(2,1)S(1)} %bitcast.102, s32[64]{0:T(128)S(1)} %eq.165), kind=kOutput, calls=%fused_computation.16 | convolution fusion | flops 12583168 | bytes 3539200 | tf_op jit(solution)/shard_map/rs,syc->ryc/dot_general | solution.py:167
  241.2 0.9 pad_maximum_fusion.2
  (53 shorter events, 2.7 us)
Async XLA Ops:
  7.2 123.3 %all-gather.2.cloned.1.call-start = ((), (), s32[]{:S(2)}) async-start(), calls=%async_computation.5 | async-start | bytes 5406720 | tf_op jit(solution)/shard_map/all_gather | solution.py:73
  12.7 22.9 %all-to-all-start = ((s32[32,1,2]{2,1,0:T(1,128)}), s32[32,1,2]{2,1,0:T(1,128)S(1)}, u32[]{:S(2)}, u32[]{:S(2)}) async-start(s32[32,1,2]{2,1,0:T(1,128)} %bitcast.1), calls=%async_computation | async-start | bytes 32768 | tf_op jit(solution)/shard_map/all_to_all | solution.py:62
  38.9 4.9 %copy-start.10 = (f32[1,32,1024]{2,1,0:T(8,128)S(1)}, f32[1,32,1024]{2,1,0:T(8,128)}, u32[]{:S(2)}) copy-start(f32[1,32,1024]{2,1,0:T(8,128)} %param.6) | copy-start | bytes 393220
  38.9 4.9 %copy-start.12 = (s32[24]{0:T(128)S(1)}, s32[24]{0:T(128)}, u32[]{:S(2)}) copy-start(s32[24]{0:T(128)} %param.9) | copy-start | bytes 292
  38.9 5.1 %copy-start.11 = (s32[24,1]{0,1:T(1,128)S(1)}, s32[24,1]{0,1:T(1,128)}, u32[]{:S(2)}) copy-start(s32[24,1]{0,1:T(1,128)} %param.7) | copy-start | bytes 292
  38.9 47.6 %all-to-all-start.1 = ((bf16[32,64,384]{2,1,0:T(8,128)(2,1)}), bf16[32,64,384]{2,1,0:T(8,128)(2,1)}, u32[]{:S(2)}, u32[]{:S(2)}) async-start(bf16[32,64,384]{2,1,0:T(8,128)(2,1)} %bitcast.3), calls=%async_computation.1 | async-start | bytes 3145728 | tf_op jit(solution)/shard_map/all_to_all | solution.py:66
  43.7 5.4 %collective-permute-start = (f32[1,32,1024]{2,1,0:T(8,128)S(1)}, f32[1,32,1024]{2,1,0:T(8,128)S(1)}, u32[]{:S(2)}, u32[]{:S(2)}) collective-permute-start(f32[1,32,1024]{2,1,0:T(8,128)S(1)} %copy-done.10), channel_id=1, source_target_pairs={{32,0},{64,32},{96,64},{128,96},{160,128},{192,160},{224,192},{256... | collective-permute-start | bytes 393224 | tf_op jit(solution)/shard_map/ppermute | solution.py:13
  54.6 35.2 %copy-start = (bf16[1024,1024]{1,0:T(8,128)(2,1)S(1)}, bf16[1024,1024]{1,0:T(8,128)(2,1)}, u32[]{:S(2)}) copy-start(bf16[1024,1024]{1,0:T(8,128)(2,1)} %get-tuple-element.6) | copy-start | bytes 6291460
  88.6 1.8 copy-start.5
  89.0 0.9 copy-start.3
  92.4 9.6 %copy-start.7 = (bf16[768,256]{1,0:T(8,128)(2,1)}, bf16[768,256]{1,0:T(8,128)(2,1)S(1)}, u32[]{:S(2)}) copy-start(bf16[768,256]{1,0:T(8,128)(2,1)S(1)} %slice.69) | copy-start | bytes 1179652
  95.4 6.5 %copy-start.9 = (bf16[768,256]{1,0:T(8,128)(2,1)S(1)}, bf16[768,256]{1,0:T(8,128)(2,1)}, u32[]{:S(2)}) copy-start(bf16[768,256]{1,0:T(8,128)(2,1)} %slice.92) | copy-start | bytes 1179652
  95.5 53.4 %all-to-all-start.2 = ((bf16[32,64,256]{2,1,0:T(8,128)(2,1)}), bf16[32,64,256]{2,1,0:T(8,128)(2,1)}, u32[]{:S(2)}, u32[]{:S(2)}) async-start(bf16[32,64,256]{2,1,0:T(8,128)(2,1)} %bitcast.109), calls=%async_computation.2 | async-start | bytes 2097152 | tf_op jit(solution)/shard_map/all_to_all | solution.py:117
  134.6 1.8 copy-start.2
  137.1 1.4 copy-start.4
  138.5 1.6 copy-start.6
  140.1 1.7 copy-start.1
  143.3 4.2 %copy-start.8 = (bf16[768,256]{1,0:T(8,128)(2,1)S(1)}, bf16[768,256]{1,0:T(8,128)(2,1)}, u32[]{:S(2)}) copy-start(bf16[768,256]{1,0:T(8,128)(2,1)} %copy-done.7) | copy-start | bytes 1179652
  148.9 17.0 %all-to-all-start.4 = ((f32[32,2,128]{2,1,0:T(2,128)}), f32[32,2,128]{2,1,0:T(2,128)S(1)}, u32[]{:S(2)}, u32[]{:S(2)}) async-start(f32[32,2,128]{2,1,0:T(2,128)} %bitcast.41), calls=%async_computation.4 | async-start | bytes 65536 | tf_op jit(solution)/shard_map/all_to_all | solution.py:159
  165.9 71.9 %all-to-all-start.3 = ((bf16[32,64,768]{2,1,0:T(8,128)(2,1)}), bf16[32,64,768]{2,1,0:T(8,128)(2,1)S(1)}, u32[]{:S(2)}, u32[]{:S(2)}) async-start(bf16[32,64,768]{2,1,0:T(8,128)(2,1)} %bitcast.101), calls=%async_computation.3 | async-start | bytes 6291456 | tf_op jit(solution)/shard_map/all_to_all | solution.py:117
Sparse Core Ops, SparseCore 0:
  11.1 119.3 all-gather.1

commit v6 on v5

--- a/solution.py
+++ b/solution.py
@@ -156,7 +156,10 @@
     send_ham = jnp.dot(
         place_hot.astype(jnp.float32), weighted, precision=lax.Precision.HIGHEST
     ).reshape(domain_count, capacity, group_size)
-    got_ham = lax.all_to_all(send_ham, "dom", split_axis=0, concat_axis=0, tiled=True).reshape(
+    shared_ham = lax.all_gather(send_ham, "dom", axis=0, tiled=True).reshape(
+        domain_count, domain_count, capacity, group_size
+    )
+    got_ham = lax.dynamic_slice_in_dim(shared_ham, lax.axis_index("dom"), 1, axis=1).reshape(
         domain_count * capacity, group_size
     )
     row_hot = asked_of_me[None, :] == jnp.arange(owned_count, dtype=jnp.int32)[:, None]

time: 250 us -> 263 us (1.052)
  waiting for transfers between devices: 142 us -> 156 us
  starting transfers between devices: 36 us -> 30.7 us
  matrix products: 22.9 us -> 26.3 us
    all_gather x0 -> x1, waiting for transfers between devices: none -> 84.9 us  [on_device(): lax.all_gather(send_ham, 'dom', axis=0, tiled=True)]
    all_to_all x2, waiting for transfers between devices: 65 us -> 0.01 us  [send_gradient(): got = lax.all_to_all(send, 'dom', split_axis=0, concat_axis=0, tiled=True)]
    all_to_all x1 -> x0, starting transfers between devices: 7.12 us -> none  [on_device(): lax.all_to_all(send_ham, 'dom', split_axis=0, concat_axis=0, tiled=True)]
    all_to_all x1 -> x0, waiting for transfers between devices: 7.05 us -> none  [on_device(): lax.all_to_all(send_ham, 'dom', split_axis=0, concat_axis=0, tiled=True)]
  transfers between devices with their start and end apart: 7 -> 7, of which waited for: 5 -> 4; matrix products, arithmetic and copies ran while one was open for 20% -> 20% of each run, Pallas kernels for 0% -> 0%
where the time goes in v6:
time: 263 us; the launch traced here: 262 us
  waiting for transfers between devices  156 us (59%)
  starting transfers between devices  30.7 us (12%)
  matrix products  26.3 us (10%)
  local copies, waits for them, and re-layouts  24.4 us (9%)
  between operations  14.4 us (5%)
  other arithmetic  10.4 us (4%)
    all_gather x1, waiting for transfers between devices, on_device(): lax.all_gather(send_ham, 'dom', axis=0, tiled=True)  84.9 us
    all_to_all x1, waiting for transfers between devices, on_device(): lax.all_to_all(lent.reshape(domain_count, capacity * NB, half), 'dom', sp...  31.8 us
    all_gather x1, waiting for transfers between devices, on_device(): gathered_b = lax.all_gather(blocks[:, :, half:], 'dom', axis=0, tiled=True)  29.3 us
    all_to_all x1, starting transfers between devices, on_device(): lax.all_to_all(asked_rows.reshape(domain_count, capacity), 'dom', split_a...  13.2 us
    all_to_all x2, starting transfers between devices, send_gradient(): got = lax.all_to_all(send, 'dom', split_axis=0, concat_axis=0, tiled=True)  12.4 us
    all_to_all x1, waiting for transfers between devices, on_device(): lax.all_to_all(asked_rows.reshape(domain_count, capacity), 'dom', split_a...  9.79 us
    dot_general x2, matrix products, on_device(): jnp.einsum('rs,syc->ryc', row_low, got, preferred_element_type=jnp.float32)  5.29 us
  transfers between devices with their start and end apart: 7, of which 4 were waited for; matrix products, arithmetic and copies ran while one was open for 20% of the time, Pallas kernels for 0%

profile of v6, /device:TPU:8, one launch (start us, length us, event | category | flops | bytes accessed | tf_op | source)
XLA Modules:
  0.0 262.1 jit_solution(7404606335301038552)
XLA Ops:
  7.2 1.0 copy.73
  8.2 0.7 slice.70
  9.0 0.7 fusion.56
  9.7 0.8 select_reduce_fusion.2
  10.6 0.7 multiply_add_fusion.2
  11.2 0.7 select_reduce_fusion
  12.0 0.7 add.111
  12.7 13.2 %all-to-all-start = ((s32[32,1,2]{2,1,0:T(1,128)}), s32[32,1,2]{2,1,0:T(1,128)S(1)}, u32[]{:S(2)}, u32[]{:S(2)}) async-start(s32[32,1,2]{2,1,0:T(1,128)} %bitcast.1), calls=%async_computation | async-start | bytes 32768 | tf_op jit(solution)/shard_map/all_to_all | solution.py:62
  25.9 9.8 %all-to-all-done = s32[32,1,2]{2,1,0:T(1,128)S(1)} async-done(((s32[32,1,2]{2,1,0:T(1,128)}), s32[32,1,2]{2,1,0:T(1,128)S(1)}, u32[]{:S(2)}, u32[]{:S(2)}) %all-to-all-start) | async-done | bytes 288 | tf_op jit(solution)/shard_map/all_to_all | solution.py:62
  35.7 0.5 broadcast.247
  36.2 0.7 reduce.3
  37.0 1.9 gather_fusion
  39.0 4.8 %all-to-all-start.1 = ((bf16[32,64,384]{2,1,0:T(8,128)(2,1)}), bf16[32,64,384]{2,1,0:T(8,128)(2,1)}, u32[]{:S(2)}, u32[]{:S(2)}) async-start(bf16[32,64,384]{2,1,0:T(8,128)(2,1)} %bitcast.3), calls=%async_computation.1 | async-start | bytes 3145728 | tf_op jit(solution)/shard_map/all_to_all | solution.py:66
  44.1 5.1 %add_convert_fusion = (bf16[1024,1024]{1,0:T(8,128)(2,1)}, bf16[1024,1024]{1,0:T(8,128)(2,1)}) fusion(s32[1024]{0:T(1024)S(1)} %get-tuple-element.14, s32[1024]{0:T(1024)S(1)} %get-tuple-element.15, s32[1024]{0:T(1024)S(1)} %get-tuple-element.13, s32[1024]{0:T(1024)S(1)} %get-tuple-element.16, pred[1024]{0:T(1024)(128)(4,1)S(1)} %get-tuple-element.17, ...), kind=kLoop, calls=%fused_computation.6 | loop fusion | flops 27262976 | bytes 4212736 | tf_op jit(solution)/shard_map/convert_element_type | solution.py:35
  49.3 2.6 gather_fusion.2
  51.9 1.2 slice.67
  53.1 1.7 slice.73
  54.7 31.8 %all-to-all-done.1 = bf16[32,64,384]{2,1,0:T(8,128)(2,1)} async-done(((bf16[32,64,384]{2,1,0:T(8,128)(2,1)}), bf16[32,64,384]{2,1,0:T(8,128)(2,1)}, u32[]{:S(2)}, u32[]{:S(2)}) %all-to-all-start.1) | async-done | bytes 1572896 | tf_op jit(solution)/shard_map/all_to_all | solution.py:66
  86.5 2.1 gather_fusion.1
  89.4 0.4 copy-done.3
  89.8 0.5 fusion.51
  90.3 1.4 bitcast_multiply_fusion.1
  91.7 1.5 fusion.20
  93.3 0.4 convolution_convert_fusion.6
  93.9 1.6 gather_fusion.3
  95.5 6.4 %all-to-all-start.2 = ((bf16[32,64,256]{2,1,0:T(8,128)(2,1)}), bf16[32,64,256]{2,1,0:T(8,128)(2,1)}, u32[]{:S(2)}, u32[]{:S(2)}) async-start(bf16[32,64,256]{2,1,0:T(8,128)(2,1)} %bitcast.110), calls=%async_computation.2 | async-start | bytes 2097152 | tf_op jit(solution)/shard_map/all_to_all | solution.py:117
  101.8 29.3 %all-gather.3.cloned.1.call-done = bf16[128,32,640]{2,1,0:T(8,128)(2,1)} async-done(((bf16[4,32,640]{2,1,0:T(8,128)(2,1)}), bf16[128,32,640]{2,1,0:T(8,128)(2,1)}) %all-gather.3.cloned.1.call-update) | async-done | bytes 5242896 | tf_op jit(solution)/shard_map/all_gather | solution.py:73
  131.2 4.2 %gather_fusion.4 = bf16[24,32,640]{2,1,0:T(8,128)(2,1)} fusion(bf16[128,32,640]{2,1,0:T(8,128)(2,1)} %all-gather.3.cloned.1.call-done, s32[1024]{0:T(1024)S(1)} %pad_clamp_fusion), kind=kCustom, calls=%fused_computation.4 | custom fusion | bytes 1966176 | tf_op jit(solution)/shard_map/jit(_take)/gather | solution.py:75
  135.3 1.8 fusion.18
  137.1 0.5 fusion.19
  138.1 1.4 copy-done.6
  139.4 1.4 fusion.6
  140.8 2.4 fusion.131
  143.3 1.5 fusion.5
  144.8 1.4 fusion.12
  146.2 0.4 fusion.16
  146.7 2.4 gather_fusion.5
  149.1 6.0 %all-to-all-start.3 = ((bf16[32,64,768]{2,1,0:T(8,128)(2,1)}), bf16[32,64,768]{2,1,0:T(8,128)(2,1)S(1)}, u32[]{:S(2)}, u32[]{:S(2)}) async-start(bf16[32,64,768]{2,1,0:T(8,128)(2,1)} %bitcast.102), calls=%async_computation.3 | async-start | bytes 6291456 | tf_op jit(solution)/shard_map/all_to_all | solution.py:117
  155.4 1.0 slice.92
  156.4 0.6 convolution_bitcast_fusion
  157.0 4.5 %fusion.39 = f32[24,24]{1,0:T(8,128)S(1)} fusion(f32[24,24]{1,0:T(8,128)S(1)} %convolution_bitcast_fusion, bf16[24,32,768]{2,1,0:T(8,128)(2,1)} %bitcast.115, bf16[24,32,768]{2,1,0:T(8,128)(2,1)} %bitcast.129), kind=kOutput, calls=%fused_computation.56 | convolution fusion | flops 28312704 | bytes 2363904 | tf_op jit(solution)/shard_map/dot_general | solution.py:142
  161.7 0.9 fusion.55
  162.6 1.9 fusion.44
  164.5 84.9 %all-gather.5.cloned.1.call-done = f32[1024,2,128]{2,1,0:T(2,128)} async-done(((f32[32,2,128]{2,1,0:T(2,128)}), f32[1024,2,128]{2,1,0:T(2,128)}) %all-gather.5.cloned.1.call-update) | async-done | bytes 1048592 | tf_op jit(solution)/shard_map/all_gather | solution.py:159
  249.4 0.8 constant_dynamic-slice_fusion
  250.1 0.7 fusion.92
  250.9 3.4 %fusion.2 = f32[4,32,768]{2,0,1:T(4,128)S(1)} fusion(bf16[64,32,768]{2,1,0:T(8,128)(2,1)S(1)} %bitcast.103, s32[64]{0:T(128)S(1)} %eq.165), kind=kOutput, calls=%fused_computation.16 | convolution fusion | flops 12583168 | bytes 3539200 | tf_op jit(solution)/shard_map/rs,syc->ryc/dot_general | solution.py:170
  254.3 0.9 pad_maximum_fusion.2
  (55 shorter events, 2.4 us)
Async XLA Ops:
  7.2 124.0 %all-gather.3.cloned.1.call-start = ((), (), s32[]{:S(2)}) async-start(), calls=%async_computation.4 | async-start | bytes 5406720 | tf_op jit(solution)/shard_map/all_gather | solution.py:73
  11.2 38.0 %copy-start.10 = (s32[24]{0:T(128)}, s32[24]{0:T(128)S(1)}, u32[]{:S(2)}) copy-start(s32[24]{0:T(128)S(1)} %get-tuple-element.8) | copy-start | bytes 292
  12.7 23.0 %all-to-all-start = ((s32[32,1,2]{2,1,0:T(1,128)}), s32[32,1,2]{2,1,0:T(1,128)S(1)}, u32[]{:S(2)}, u32[]{:S(2)}) async-start(s32[32,1,2]{2,1,0:T(1,128)} %bitcast.1), calls=%async_computation | async-start | bytes 32768 | tf_op jit(solution)/shard_map/all_to_all | solution.py:62
  38.9 4.8 %copy-start.8 = (f32[1,32,1024]{2,1,0:T(8,128)S(1)}, f32[1,32,1024]{2,1,0:T(8,128)}, u32[]{:S(2)}) copy-start(f32[1,32,1024]{2,1,0:T(8,128)} %param.6) | copy-start | bytes 393220
  39.0 4.9 %copy-start.12 = (s32[24]{0:T(128)S(1)}, s32[24]{0:T(128)}, u32[]{:S(2)}) copy-start(s32[24]{0:T(128)} %param.9) | copy-start | bytes 292
  39.0 5.1 %copy-start.9 = (s32[24,1]{0,1:T(1,128)S(1)}, s32[24,1]{0,1:T(1,128)}, u32[]{:S(2)}) copy-start(s32[24,1]{0,1:T(1,128)} %param.7) | copy-start | bytes 292
  39.0 47.5 %all-to-all-start.1 = ((bf16[32,64,384]{2,1,0:T(8,128)(2,1)}), bf16[32,64,384]{2,1,0:T(8,128)(2,1)}, u32[]{:S(2)}, u32[]{:S(2)}) async-start(bf16[32,64,384]{2,1,0:T(8,128)(2,1)} %bitcast.3), calls=%async_computation.1 | async-start | bytes 3145728 | tf_op jit(solution)/shard_map/all_to_all | solution.py:66
  43.8 5.4 %collective-permute-start = (f32[1,32,1024]{2,1,0:T(8,128)S(1)}, f32[1,32,1024]{2,1,0:T(8,128)S(1)}, u32[]{:S(2)}, u32[]{:S(2)}) collective-permute-start(f32[1,32,1024]{2,1,0:T(8,128)S(1)} %copy-done.8), channel_id=1, source_target_pairs={{32,0},{64,32},{96,64},{128,96},{160,128},{192,160},{224,192},{256... | collective-permute-start | bytes 393224 | tf_op jit(solution)/shard_map/ppermute | solution.py:13
  54.7 35.1 %copy-start = (bf16[1024,1024]{1,0:T(8,128)(2,1)S(1)}, bf16[1024,1024]{1,0:T(8,128)(2,1)}, u32[]{:S(2)}) copy-start(bf16[1024,1024]{1,0:T(8,128)(2,1)} %get-tuple-element.6) | copy-start | bytes 6291460
  88.6 1.7 copy-start.5
  89.0 0.8 copy-start.3
  95.5 53.6 %all-to-all-start.2 = ((bf16[32,64,256]{2,1,0:T(8,128)(2,1)}), bf16[32,64,256]{2,1,0:T(8,128)(2,1)}, u32[]{:S(2)}, u32[]{:S(2)}) async-start(bf16[32,64,256]{2,1,0:T(8,128)(2,1)} %bitcast.110), calls=%async_computation.2 | async-start | bytes 2097152 | tf_op jit(solution)/shard_map/all_to_all | solution.py:117
  135.3 1.8 copy-start.2
  135.3 2.3 copy-start.4
  137.8 1.6 copy-start.6
  140.8 2.4 copy-start.1
  144.8 1.4 copy-start.7
  149.1 101.8 %all-to-all-start.3 = ((bf16[32,64,768]{2,1,0:T(8,128)(2,1)}), bf16[32,64,768]{2,1,0:T(8,128)(2,1)S(1)}, u32[]{:S(2)}, u32[]{:S(2)}) async-start(bf16[32,64,768]{2,1,0:T(8,128)(2,1)} %bitcast.102), calls=%async_computation.3 | async-start | bytes 6291456 | tf_op jit(solution)/shard_map/all_to_all | solution.py:117
  155.1 94.3 %all-gather.5.cloned.1.call-start = ((), (), s32[]{:S(2)}) async-start(), calls=%async_computation.5 | async-start | bytes 1081344 | tf_op jit(solution)/shard_map/all_gather | solution.py:159
  156.4 5.1 %copy-start.11 = (s32[24]{0:T(128)S(1)}, s32[24]{0:T(128)}, u32[]{:S(2)}) copy-start(s32[24]{0:T(128)} %copy-done.10) | copy-start | bytes 292
Sparse Core Ops, SparseCore 0:
  11.7 119.3 all-gather.2
  162.7 86.5 all-gather.4

commit v7 on v6

--- a/solution.py
+++ b/solution.py
@@ -159,11 +159,16 @@
     shared_ham = lax.all_gather(send_ham, "dom", axis=0, tiled=True).reshape(
         domain_count, domain_count, capacity, group_size
     )
-    got_ham = lax.dynamic_slice_in_dim(shared_ham, lax.axis_index("dom"), 1, axis=1).reshape(
-        domain_count * capacity, group_size
+    row_hot = asked_of_me[None, :] == jnp.arange(owned_count, dtype=jnp.int32)[:, None]
+    mine = lax.axis_index("dom") == jnp.arange(domain_count, dtype=jnp.int32)
+    pick_ham = (
+        row_hot.reshape(owned_count, domain_count, 1, capacity) & mine[None, None, :, None]
+    ).astype(jnp.float32)
+    hamilton = jnp.dot(
+        pick_ham.reshape(owned_count, -1),
+        shared_ham.reshape(-1, group_size),
+        precision=lax.Precision.HIGHEST,
     )
-    row_hot = asked_of_me[None, :] == jnp.arange(owned_count, dtype=jnp.int32)[:, None]
-    hamilton = jnp.dot(row_hot.astype(jnp.float32), got_ham, precision=lax.Precision.HIGHEST)
     row_low = row_hot.astype(jnp.bfloat16)
     gradient = jnp.concatenate(
         [

time: 263 us -> 265 us (level)
  waiting for transfers between devices: 156 us -> 148 us
  other arithmetic: 10.4 us -> 13.9 us
  local copies, waits for them, and re-layouts: 24.4 us -> 27.4 us
    all_gather x1, waiting for transfers between devices: 84.9 us -> 80.8 us  [on_device(): lax.all_gather(send_ham, 'dom', axis=0, tiled=True)]
  transfers between devices with their start and end apart: 7 -> 7, of which waited for: 4 -> 4; matrix products, arithmetic and copies ran while one was open for 20% -> 23% of each run, Pallas kernels for 0% -> 0%
where the time goes in v7:
time: 265 us; the launch traced here: 264 us
  waiting for transfers between devices  148 us (56%)
  starting transfers between devices  32.2 us (12%)
  matrix products  27.8 us (10%)
  local copies, waits for them, and re-layouts  27.4 us (10%)
  between operations  14.4 us (5%)
  other arithmetic  13.9 us (5%)
    all_gather x1, waiting for transfers between devices, on_device(): lax.all_gather(send_ham, 'dom', axis=0, tiled=True)  80.8 us
    all_to_all x1, waiting for transfers between devices, on_device(): lax.all_to_all(lent.reshape(domain_count, capacity * NB, half), 'dom', sp...  29.1 us
    all_gather x1, waiting for transfers between devices, on_device(): gathered_b = lax.all_gather(blocks[:, :, half:], 'dom', axis=0, tiled=True)  28.6 us
    all_to_all x2, starting transfers between devices, send_gradient(): got = lax.all_to_all(send, 'dom', split_axis=0, concat_axis=0, tiled=True)  13.8 us
    all_to_all x1, starting transfers between devices, on_device(): lax.all_to_all(asked_rows.reshape(domain_count, capacity), 'dom', split_a...  13.2 us
    all_to_all x1, waiting for transfers between devices, on_device(): lax.all_to_all(asked_rows.reshape(domain_count, capacity), 'dom', split_a...  9.79 us
  transfers between devices with their start and end apart: 7, of which 4 were waited for; matrix products, arithmetic and copies ran while one was open for 23% of the time, Pallas kernels for 0%

profile of v7, /device:TPU:8, one launch (start us, length us, event | category | flops | bytes accessed | tf_op | source)
XLA Modules:
  0.0 264.1 jit_solution(2891275782922026606)
XLA Ops:
  7.2 1.0 copy.82
  8.2 0.7 slice.70
  9.0 0.7 fusion.56
  9.7 0.8 select_reduce_fusion.2
  10.6 0.7 multiply_add_fusion.2
  11.2 0.6 copy-done.12
  11.8 0.7 select_reduce_fusion
  12.6 0.7 add.108
  13.3 13.2 %all-to-all-start = ((s32[32,1,2]{2,1,0:T(1,128)}), s32[32,1,2]{2,1,0:T(1,128)S(1)}, u32[]{:S(2)}, u32[]{:S(2)}) async-start(s32[32,1,2]{2,1,0:T(1,128)} %bitcast.1), calls=%async_computation | async-start | bytes 32768 | tf_op jit(solution)/shard_map/all_to_all | solution.py:62
  26.5 9.8 %all-to-all-done = s32[32,1,2]{2,1,0:T(1,128)S(1)} async-done(((s32[32,1,2]{2,1,0:T(1,128)}), s32[32,1,2]{2,1,0:T(1,128)S(1)}, u32[]{:S(2)}, u32[]{:S(2)}) %all-to-all-start) | async-done | bytes 288 | tf_op jit(solution)/shard_map/all_to_all | solution.py:62
  36.8 0.7 reduce.3
  37.6 1.9 gather_fusion
  39.5 4.8 %all-to-all-start.1 = ((bf16[32,64,384]{2,1,0:T(8,128)(2,1)}), bf16[32,64,384]{2,1,0:T(8,128)(2,1)}, u32[]{:S(2)}, u32[]{:S(2)}) async-start(bf16[32,64,384]{2,1,0:T(8,128)(2,1)} %bitcast.3), calls=%async_computation.1 | async-start | bytes 3145728 | tf_op jit(solution)/shard_map/all_to_all | solution.py:66
  44.6 0.6 pad_clamp_fusion.2
  45.2 0.6 pad_clamp_fusion.1
  45.8 5.1 %add_convert_fusion = (bf16[1024,1024]{1,0:T(8,128)(2,1)}, bf16[1024,1024]{1,0:T(8,128)(2,1)}) fusion(s32[1024]{0:T(1024)S(1)} %get-tuple-element.14, s32[1024]{0:T(1024)S(1)} %get-tuple-element.15, s32[1024]{0:T(1024)S(1)} %get-tuple-element.13, s32[1024]{0:T(1024)S(1)} %get-tuple-element.16, pred[1024]{0:T(1024)(128)(4,1)S(1)} %get-tuple-element.17, ...), kind=kLoop, calls=%fused_computation.6 | loop fusion | flops 27262976 | bytes 4212736 | tf_op jit(solution)/shard_map/convert_element_type | solution.py:35
  50.9 0.6 pad_clamp_fusion.3
  51.5 0.6 pad_clamp_fusion
  52.1 2.7 %gather_fusion.2 = f32[768,1024]{1,0:T(8,128)S(1)} fusion(f32[64,1024]{1,0:T(8,128)S(1)} %pad_maximum_fusion.3, s32[1024]{0:T(1024)} %pad_clamp_fusion.2), kind=kCustom, calls=%fused_computation.2 | custom fusion | bytes 6294528 | tf_op jit(solution)/shard_map/jit(_take)/gather | solution.py:79
  54.9 1.2 slice.67
  56.1 1.6 slice.73
  57.7 29.1 %all-to-all-done.1 = bf16[32,64,384]{2,1,0:T(8,128)(2,1)} async-done(((bf16[32,64,384]{2,1,0:T(8,128)(2,1)}), bf16[32,64,384]{2,1,0:T(8,128)(2,1)}, u32[]{:S(2)}, u32[]{:S(2)}) %all-to-all-start.1) | async-done | bytes 1572896 | tf_op jit(solution)/shard_map/all_to_all | solution.py:66
  86.8 2.2 gather_fusion.1
  90.8 1.4 bitcast_multiply_fusion.1
  92.2 1.5 fusion.20
  94.3 1.7 gather_fusion.3
  96.0 6.7 %all-to-all-start.2 = ((bf16[32,64,256]{2,1,0:T(8,128)(2,1)}), bf16[32,64,256]{2,1,0:T(8,128)(2,1)}, u32[]{:S(2)}, u32[]{:S(2)}) async-start(bf16[32,64,256]{2,1,0:T(8,128)(2,1)} %bitcast.113), calls=%async_computation.2 | async-start | bytes 2097152 | tf_op jit(solution)/shard_map/all_to_all | solution.py:117
  102.7 28.6 %all-gather.3.cloned.1.call-done = bf16[128,32,640]{2,1,0:T(8,128)(2,1)} async-done(((bf16[4,32,640]{2,1,0:T(8,128)(2,1)}), bf16[128,32,640]{2,1,0:T(8,128)(2,1)}) %all-gather.3.cloned.1.call-update) | async-done | bytes 5242896 | tf_op jit(solution)/shard_map/all_gather | solution.py:73
  131.3 4.3 %gather_fusion.4 = bf16[24,32,640]{2,1,0:T(8,128)(2,1)} fusion(bf16[128,32,640]{2,1,0:T(8,128)(2,1)} %all-gather.3.cloned.1.call-done, s32[1024]{0:T(1024)} %pad_clamp_fusion), kind=kCustom, calls=%fused_computation.4 | custom fusion | bytes 1966176 | tf_op jit(solution)/shard_map/jit(_take)/gather | solution.py:75
  135.6 1.8 fusion.18
  138.3 1.4 copy-done.6
  139.7 1.4 fusion.6
  141.1 2.4 fusion.129
  143.5 1.5 fusion.5
  145.0 1.4 fusion.12
  146.9 2.5 gather_fusion.5
  149.4 7.1 %all-to-all-start.3 = ((bf16[32,64,768]{2,1,0:T(8,128)(2,1)}), bf16[32,64,768]{2,1,0:T(8,128)(2,1)S(1)}, u32[]{:S(2)}, u32[]{:S(2)}) async-start(bf16[32,64,768]{2,1,0:T(8,128)(2,1)} %bitcast.105), calls=%async_computation.3 | async-start | bytes 6291456 | tf_op jit(solution)/shard_map/all_to_all | solution.py:117
  156.8 1.0 slice.92
  157.9 0.6 convolution_bitcast_fusion
  158.5 4.5 %fusion.39 = f32[24,24]{1,0:T(8,128)S(1)} fusion(f32[24,24]{1,0:T(8,128)S(1)} %convolution_bitcast_fusion, bf16[24,32,768]{2,1,0:T(8,128)(2,1)} %bitcast.118, bf16[24,32,768]{2,1,0:T(8,128)(2,1)} %bitcast.132), kind=kOutput, calls=%fused_computation.56 | convolution fusion | flops 28312704 | bytes 2363904 | tf_op jit(solution)/shard_map/dot_general | solution.py:142
  163.2 0.9 fusion.55
  164.2 1.1 broadcast_and_fusion
  165.3 2.6 and.74
  167.9 1.9 fusion.44
  169.8 80.8 %all-gather.5.cloned.1.call-done = f32[1024,2,128]{2,1,0:T(2,128)} async-done(((f32[32,2,128]{2,1,0:T(2,128)}), f32[1024,2,128]{2,1,0:T(2,128)}) %all-gather.5.cloned.1.call-update) | async-done | bytes 1048592 | tf_op jit(solution)/shard_map/all_gather | solution.py:159
  250.7 2.3 fusion.130
  252.9 3.4 %fusion.2 = f32[4,32,768]{2,0,1:T(4,128)S(1)} fusion(bf16[64,32,768]{2,1,0:T(8,128)(2,1)S(1)} %bitcast.106, s32[64]{0:T(128)S(1)} %copy-done.10), kind=kOutput, calls=%fused_computation.16 | convolution fusion | flops 12583168 | bytes 3539200 | tf_op jit(solution)/shard_map/rs,syc->ryc/dot_general | solution.py:175
  256.3 0.9 pad_maximum_fusion.2
  (66 shorter events, 5.1 us)
Async XLA Ops:
  7.2 124.1 %all-gather.3.cloned.1.call-start = ((), (), s32[]{:S(2)}) async-start(), calls=%async_computation.4 | async-start | bytes 5406720 | tf_op jit(solution)/shard_map/all_gather | solution.py:73
  11.2 0.6 copy-start.12
  11.2 40.3 %copy-start.14 = (s32[24]{0:T(128)}, s32[24]{0:T(128)S(1)}, u32[]{:S(2)}) copy-start(s32[24]{0:T(128)S(1)} %get-tuple-element.8) | copy-start | bytes 292
  13.3 23.0 %all-to-all-start = ((s32[32,1,2]{2,1,0:T(1,128)}), s32[32,1,2]{2,1,0:T(1,128)S(1)}, u32[]{:S(2)}, u32[]{:S(2)}) async-start(s32[32,1,2]{2,1,0:T(1,128)} %bitcast.1), calls=%async_computation | async-start | bytes 32768 | tf_op jit(solution)/shard_map/all_to_all | solution.py:62
  37.6 1.9 copy-start.9
  39.5 4.9 %copy-start.8 = (f32[1,32,1024]{2,1,0:T(8,128)S(1)}, f32[1,32,1024]{2,1,0:T(8,128)}, u32[]{:S(2)}) copy-start(f32[1,32,1024]{2,1,0:T(8,128)} %param.6) | copy-start | bytes 393220
  39.5 4.9 %copy-start.16 = (s32[24]{0:T(128)S(1)}, s32[24]{0:T(128)}, u32[]{:S(2)}) copy-start(s32[24]{0:T(128)} %param.9) | copy-start | bytes 292
  39.5 6.3 %copy-start.11 = (s32[24,1]{0,1:T(1,128)S(1)}, s32[24,1]{0,1:T(1,128)}, u32[]{:S(2)}) copy-start(s32[24,1]{0,1:T(1,128)} %param.7) | copy-start | bytes 292
  39.5 47.3 %all-to-all-start.1 = ((bf16[32,64,384]{2,1,0:T(8,128)(2,1)}), bf16[32,64,384]{2,1,0:T(8,128)(2,1)}, u32[]{:S(2)}, u32[]{:S(2)}) async-start(bf16[32,64,384]{2,1,0:T(8,128)(2,1)} %bitcast.3), calls=%async_computation.1 | async-start | bytes 3145728 | tf_op jit(solution)/shard_map/all_to_all | solution.py:66
  44.4 7.7 %collective-permute-start = (f32[1,32,1024]{2,1,0:T(8,128)S(1)}, f32[1,32,1024]{2,1,0:T(8,128)S(1)}, u32[]{:S(2)}, u32[]{:S(2)}) collective-permute-start(f32[1,32,1024]{2,1,0:T(8,128)S(1)} %copy-done.8), channel_id=1, source_target_pairs={{32,0},{64,32},{96,64},{128,96},{160,128},{192,160},{224,192},{256... | collective-permute-start | bytes 393224 | tf_op jit(solution)/shard_map/ppermute | solution.py:13
  57.7 32.5 %copy-start = (bf16[1024,1024]{1,0:T(8,128)(2,1)S(1)}, bf16[1024,1024]{1,0:T(8,128)(2,1)}, u32[]{:S(2)}) copy-start(bf16[1024,1024]{1,0:T(8,128)(2,1)} %get-tuple-element.6) | copy-start | bytes 6291460
  89.0 1.7 copy-start.5
  89.4 0.8 copy-start.3
  96.0 53.4 %all-to-all-start.2 = ((bf16[32,64,256]{2,1,0:T(8,128)(2,1)}), bf16[32,64,256]{2,1,0:T(8,128)(2,1)}, u32[]{:S(2)}, u32[]{:S(2)}) async-start(bf16[32,64,256]{2,1,0:T(8,128)(2,1)} %bitcast.113), calls=%async_computation.2 | async-start | bytes 2097152 | tf_op jit(solution)/shard_map/all_to_all | solution.py:117
  135.6 1.8 copy-start.2
  135.6 2.3 copy-start.4
  138.1 1.6 copy-start.6
  141.1 2.4 copy-start.1
  145.0 1.4 copy-start.7
  149.4 103.5 %all-to-all-start.3 = ((bf16[32,64,768]{2,1,0:T(8,128)(2,1)}), bf16[32,64,768]{2,1,0:T(8,128)(2,1)S(1)}, u32[]{:S(2)}, u32[]{:S(2)}) async-start(bf16[32,64,768]{2,1,0:T(8,128)(2,1)} %bitcast.105), calls=%async_computation.3 | async-start | bytes 6291456 | tf_op jit(solution)/shard_map/all_to_all | solution.py:117
  156.6 94.1 %all-gather.5.cloned.1.call-start = ((), (), s32[]{:S(2)}) async-start(), calls=%async_computation.5 | async-start | bytes 1081344 | tf_op jit(solution)/shard_map/all_gather | solution.py:159
  157.9 5.1 %copy-start.15 = (s32[24]{0:T(128)S(1)}, s32[24]{0:T(128)}, u32[]{:S(2)}) copy-start(s32[24]{0:T(128)} %copy-done.14) | copy-start | bytes 292
  157.9 5.3 %copy-start.13 = (s32[24]{0:T(128)S(1)}, s32[24]{0:T(128)}, u32[]{:S(2)}) copy-start(s32[24]{0:T(128)} %copy-done.12) | copy-start | bytes 292
  158.5 9.5 %copy-start.10 = (s32[64]{0:T(128)S(1)}, s32[64]{0:T(128)}, u32[]{:S(2)}) copy-start(s32[64]{0:T(128)} %copy-done.9) | copy-start | bytes 772
Sparse Core Ops, SparseCore 0:
  11.7 119.5 all-gather.2
  164.2 86.3 all-gather.4
